TPU v7x, 256 devices: a whole 4x4x8 slice. The times are simulated.
256 devices in a mesh: depth: 16 (over y_hi, z), filt: 16 (over x, y_lo, core).
Axes of the slice: x: 4, y: 4 (y_hi: 2, y_lo: 2; y = y_hi * 2 + y_lo), z: 8, core: 2. Of those that a mesh axis runs over, the one named last changes fastest.
Arguments:
- features: bfloat16 [32, 128, 4096], P('depth', 'filt'), may hold values from -6 to 6
- first_kernel: bfloat16 [3, 3, 3, 256, 128], P(None, None, None, 'filt'), may hold values from -0.109375 to 0.109375
- first_bias: float32 [256], P('filt'), may hold values from -1.5 to 1.5
- second_kernel: bfloat16 [3, 3, 3, 256, 256], P(None, None, None, 'filt'), may hold values from -0.078125 to 0.078125
- second_bias: float32 [256], P('filt'), may hold values from -1.5 to 1.5
Outputs:
- activated: bfloat16 [32, 256, 4096], P('depth', 'filt')
All inputs are finite; a program needn't handle non-finite values.
Results may differ from a plain program's by a relative error of at most 0.0047.
Values may be sent and summed in bfloat16 or wider, within the bound.
No kernel may reach another device: no remote copies, remote signals or barrier semaphores. Data moves between devices by JAX's collectives and lax.ppermute only.
A program may use at most 64 MiB of HBM per device.

v0:
```python
import jax
import jax.numpy as jnp
from jax import lax
from jax.sharding import PartitionSpec as P

SIDE = 64


leak_slope = 0.3


def activate(summed, bias):
    shifted = summed + bias[None, :, None, None]
    return jnp.where(shifted > 0, shifted, leak_slope * shifted).astype(jnp.bfloat16)


def conv(framed, kernel):
    summed = lax.conv_general_dilated(
        framed[None],
        kernel,
        (1, 1, 1),
        ((0, 0), (0, 0), (1, 1)),
        dimension_numbers=("NDCHW", "DHWOI", "NDCHW"),
        preferred_element_type=jnp.float32,
    )
    return summed[0]


def depth_halo(block):
    count = lax.axis_size("depth")
    forward = [(i, i + 1) for i in range(count - 1)]
    backward = [(i + 1, i) for i in range(count - 1)]
    low = lax.ppermute(block[block.shape[0] - 1 :], "depth", forward)
    high = lax.ppermute(block[:1], "depth", backward)
    return jnp.concatenate([low, block, high], axis=0)


def row_halo(block):
    count = lax.axis_size("filt")
    forward = [(i, i + 1) for i in range(count - 1)]
    backward = [(i + 1, i) for i in range(count - 1)]
    above = lax.ppermute(block[:, :, block.shape[2] - 1 :], "filt", forward)
    below = lax.ppermute(block[:, :, :1], "filt", backward)
    return jnp.concatenate([above, block, below], axis=2)


def gather_kernels(first_kernel, second_kernel):
    count = lax.axis_size("filt")
    flat = jnp.concatenate([first_kernel.reshape(-1), second_kernel.reshape(-1)])
    whole = lax.all_gather(flat, "filt", axis=0, tiled=False)
    split = first_kernel.size
    kernels = []
    for part, kernel in ((whole[:, :split], first_kernel), (whole[:, split:], second_kernel)):
        stacked = jnp.moveaxis(part.reshape((count,) + kernel.shape), 0, 3)
        kernels.append(stacked.reshape(3, 3, 3, count * kernel.shape[3], kernel.shape[4]))
    return kernels


def gather_biases(first_bias, second_bias):
    count = lax.axis_size("filt")
    pair = jnp.stack([first_bias, second_bias])
    spread = jnp.broadcast_to(pair[None], (count,) + pair.shape)
    whole = lax.all_to_all(spread, "filt", 0, 0, tiled=True)
    return whole[:, 0].reshape(-1), whole[:, 1].reshape(-1)


def local(features, first_kernel, first_bias, second_kernel, second_bias):
    count = lax.axis_size("filt")
    planes, chans, cells = features.shape
    rows = cells // SIDE
    block_rows = rows // count
    kernel_1, kernel_2 = gather_kernels(first_kernel, second_kernel)
    bias_1, bias_2 = gather_biases(first_bias, second_bias)

    extended = depth_halo(features).reshape(planes + 2, chans, rows, SIDE)
    framed = jnp.pad(extended, ((0, 0), (0, 0), (1, 1), (0, 0)))
    windows = jnp.stack(
        [framed[:, :, b * block_rows : b * block_rows + block_rows + 2] for b in range(count)], axis=2
    )
    windows = windows.reshape(planes + 2, chans, count, (block_rows + 2) * SIDE)
    mine = lax.all_to_all(windows, "filt", 2, 1, tiled=True)
    mine = mine.reshape(planes + 2, count * chans, block_rows + 2, SIDE)

    hidden = activate(conv(mine, kernel_1), bias_1)
    second = activate(conv(row_halo(depth_halo(hidden)), kernel_2), bias_2)

    outs = second_kernel.shape[3]
    second = second.reshape(planes, count, outs, block_rows * SIDE)
    result = lax.all_to_all(second, "filt", 1, 3, tiled=True)
    return result.reshape(planes, outs, cells)


def solution(mesh):
    in_specs = (
        P("depth", "filt", None),
        P(None, None, None, "filt", None),
        P("filt"),
        P(None, None, None, "filt", None),
        P("filt"),
    )
    out_specs = P("depth", "filt", None)
    return jax.shard_map(local, mesh=mesh, in_specs=in_specs, out_specs=out_specs, check_vma=False)
```

profile of v0, /device:TPU:17, one launch (start us, length us, event | category | flops | bytes accessed | tf_op | source)
XLA Modules:
  0.0 117.7 jit_solution(16951459675588233966)
XLA Ops:
  6.5 1.1 copy.48
  7.6 1.7 %pad_maximum_fusion.1 = bf16[165888]{0:T(1024)(128)(2,1)} fusion(bf16[110592]{0:T(1024)(128)(2,1)S(1)} %bitcast.68, bf16[55296]{0:T(1024)(128)(2,1)} %bitcast.70), kind=kLoop, calls=%fused_computation.29 | loop fusion | flops 663552 | bytes 663552 | tf_op jit(solution)/shard_map/concatenate | solution.py:49
  9.3 0.9 fusion.27
  10.2 3.5 %collective-permute-start = (bf16[1,8,4096]{2,1,0:T(8,128)(2,1)S(1)}, bf16[1,8,4096]{2,1,0:T(8,128)(2,1)S(1)}, u32[]{:S(2)}, u32[]{:S(2)}) collective-permute-start(bf16[1,8,4096]{2,1,0:T(8,128)(2,1)S(1)} %get-tuple-element.25), channel_id=1, source_target_pairs={{0,16},{16,32},{32,48},{48,64},{64,80},{80,96},{96,112},{112,128},... | collective-permute-start | bytes 196616 | tf_op jit(solution)/shard_map/ppermute | solution.py:33
  13.8 5.6 %collective-permute-start.1 = (bf16[1,8,4096]{2,1,0:T(8,128)(2,1)S(1)}, bf16[1,8,4096]{2,1,0:T(8,128)(2,1)S(1)}, u32[]{:S(2)}, u32[]{:S(2)}) collective-permute-start(bf16[1,8,4096]{2,1,0:T(8,128)(2,1)S(1)} %get-tuple-element.26), channel_id=1, source_target_pairs={{16,0},{32,16},{48,32},{64,48},{80,64},{96,80},{112,96},{128,112},... | collective-permute-start | bytes 196616 | tf_op jit(solution)/shard_map/ppermute | solution.py:34
  19.4 0.7 pad_maximum_fusion.3
  20.1 0.6 broadcast_in_dim.4
  20.7 6.9 %all-to-all-start.1 = ((f32[16,2,16]{2,1,0:T(2,128)}), f32[16,2,16]{2,1,0:T(2,128)S(1)}, u32[]{:S(2)}, u32[]{:S(2)}) async-start(f32[16,2,16]{2,1,0:T(2,128)} %broadcast_in_dim.4), calls=%async_computation.1 | async-start | bytes 32768 | tf_op jit(solution)/shard_map/all_to_all | solution.py:63
  27.6 0.9 pad_maximum_fusion.2
  28.5 0.5 reshape.66
  31.4 0.6 constant_dynamic-update-slice_fusion.15
  32.0 0.6 constant_dynamic-update-slice_fusion.14
  32.6 0.6 constant_dynamic-update-slice_fusion.13
  33.2 0.6 constant_dynamic-update-slice_fusion.12
  33.8 0.6 constant_dynamic-update-slice_fusion.11
  34.4 0.6 constant_dynamic-update-slice_fusion.10
  35.0 0.6 constant_dynamic-update-slice_fusion.9
  35.6 0.6 constant_dynamic-update-slice_fusion.8
  36.2 0.6 constant_dynamic-update-slice_fusion.7
  36.9 0.6 constant_dynamic-update-slice_fusion.6
  37.5 0.6 constant_dynamic-update-slice_fusion.5
  38.1 0.6 constant_dynamic-update-slice_fusion.4
  38.7 0.6 constant_dynamic-update-slice_fusion.3
  39.3 0.6 constant_dynamic-update-slice_fusion.2
  39.9 0.6 constant_dynamic-update-slice_fusion.1
  40.5 0.6 constant_dynamic-update-slice_fusion
  41.1 5.7 %all-to-all-start = ((bf16[4,8,16,384]{3,1,0,2:T(8,128)(2,1)}), bf16[4,8,16,384]{3,1,0,2:T(8,128)(2,1)S(1)}, u32[]{:S(2)}, u32[]{:S(2)}) async-start(bf16[4,8,16,384]{3,1,0,2:T(8,128)(2,1)} %constant_dynamic-update-slice_fusion), calls=%async_computation | async-start | bytes 786432 | tf_op jit(solution)/shard_map/all_to_all | solution.py:81
  46.9 9.9 %all-to-all-done = bf16[4,8,16,384]{3,1,0,2:T(8,128)(2,1)S(1)} async-done(((bf16[4,8,16,384]{3,1,0,2:T(8,128)(2,1)}), bf16[4,8,16,384]{3,1,0,2:T(8,128)(2,1)S(1)}, u32[]{:S(2)}, u32[]{:S(2)}) %all-to-all-start) | async-done | bytes 393248 | tf_op jit(solution)/shard_map/all_to_all | solution.py:81
  56.9 0.6 reshape.88
  57.5 0.7 copy.47
  58.5 5.6 %reshape.98 = bf16[16,165888]{1,0:T(8,128)(2,1)} reshape(bf16[2654208]{0:T(1024)(128)(2,1)} %all-gather.3.cloned.1.call-done) | data formatting | bytes 10616832 | tf_op jit(solution)/shard_map/all_gather | solution.py:50
  64.1 1.6 %slice_bitcast_fusion = bf16[2,8,432,128]{3,1,2,0:T(8,128)(2,1)S(1)} fusion(bf16[16,165888]{1,0:T(8,128)(2,1)} %reshape.98), kind=kLoop, calls=%fused_computation.2 | loop fusion | bytes 3538944
  65.9 0.5 copy.35
  66.6 1.3 %convolution_select_fusion.1 = f32[2,4,8,9,256]{4,2,3,1,0:T(8,128)S(1)} fusion(bf16[3,3,3,256,128]{4,3,2,1,0:T(8,128)(2,1)S(1)} %bitcast.64, bf16[4,128,6,1,7,2]{1,4,5,2,0,3:T(8,128)(2,1)S(1)} %slice.136, bf16[4,128,6,1,8,9]{1,4,5,2,0,3:T(8,128)(2,1)S(1)} %copy.34, pred[8,9]{0,1:T(8,128)(4,1)S(1)} %copy-done), kind=kOutput, calls=%fused_computation.6 | convolution fusion | flops 1020985344 | bytes 2887752 | tf_op jit(solution)/shard_map/conv_general_dilated | solution.py:18
  68.4 3.6 %collective-permute-start.2 = (bf16[1,256,4,64]{1,2,3,0:T(4,128)(2,1)S(1)}, bf16[1,256,4,64]{1,2,3,0:T(4,128)(2,1)S(1)}, u32[]{:S(2)}, u32[]{:S(2)}) collective-permute-start(bf16[1,256,4,64]{1,2,3,0:T(4,128)(2,1)S(1)} %get-tuple-element.23), channel_id=1, source_target_pairs={{0,16},{16,32},{32,48},{48,64},{64,80},{80,96},{96,112},{112,128},... | collective-permute-start | bytes 393224 | tf_op jit(solution)/shard_map/ppermute | solution.py:33
  72.0 5.3 %collective-permute-start.3 = (bf16[1,256,4,64]{1,2,3,0:T(4,128)(2,1)S(1)}, bf16[1,256,4,64]{1,2,3,0:T(4,128)(2,1)S(1)}, u32[]{:S(2)}, u32[]{:S(2)}) collective-permute-start(bf16[1,256,4,64]{1,2,3,0:T(4,128)(2,1)S(1)} %get-tuple-element.24), channel_id=1, source_target_pairs={{16,0},{32,16},{48,32},{64,48},{80,64},{96,80},{112,96},{128,112},... | collective-permute-start | bytes 393224 | tf_op jit(solution)/shard_map/ppermute | solution.py:34
  77.3 1.3 %collective-permute-done.2 = bf16[1,256,4,64]{1,2,3,0:T(4,128)(2,1)S(1)} collective-permute-done((bf16[1,256,4,64]{1,2,3,0:T(4,128)(2,1)S(1)}, bf16[1,256,4,64]{1,2,3,0:T(4,128)(2,1)S(1)}, u32[]{:S(2)}, u32[]{:S(2)}) %collective-permute-start.2) | collective-permute-done | bytes 131104 | tf_op jit(solution)/shard_map/ppermute | solution.py:33
  78.6 0.9 collective-permute-done.3
  80.2 4.6 %collective-permute-start.4 = (bf16[4,256,1,64]{1,2,3,0:T(2,128)(2,1)S(1)}, bf16[4,256,1,64]{1,2,3,0:T(2,128)(2,1)S(1)}, u32[]{:S(2)}, u32[]{:S(2)}) collective-permute-start(bf16[4,256,1,64]{1,2,3,0:T(2,128)(2,1)S(1)} %get-tuple-element.5), channel_id=1, source_target_pairs={{0,1},{1,2},{2,3},{3,4},{4,5},{5,6},{6,7},{7,8},{8,9},{9,10},{10,1... | collective-permute-start | bytes 393224 | tf_op jit(solution)/shard_map/ppermute | solution.py:42
  84.8 2.4 %collective-permute-start.5 = (bf16[4,256,1,64]{1,2,3,0:T(2,128)(2,1)S(1)}, bf16[4,256,1,64]{1,2,3,0:T(2,128)(2,1)S(1)}, u32[]{:S(2)}, u32[]{:S(2)}) collective-permute-start(bf16[4,256,1,64]{1,2,3,0:T(2,128)(2,1)S(1)} %get-tuple-element.6), channel_id=1, source_target_pairs={{1,0},{2,1},{3,2},{4,3},{5,4},{6,5},{7,6},{8,7},{9,8},{10,9},{11,1... | collective-permute-start | bytes 393224 | tf_op jit(solution)/shard_map/ppermute | solution.py:43
  87.2 0.7 copy.50
  87.9 0.4 copy.40
  88.4 4.4 %collective-permute-done.5 = bf16[4,256,1,64]{1,2,3,0:T(2,128)(2,1)S(1)} collective-permute-done((bf16[4,256,1,64]{1,2,3,0:T(2,128)(2,1)S(1)}, bf16[4,256,1,64]{1,2,3,0:T(2,128)(2,1)S(1)}, u32[]{:S(2)}, u32[]{:S(2)}) %collective-permute-start.5) | collective-permute-done | bytes 131104 | tf_op jit(solution)/shard_map/ppermute | solution.py:43
  92.8 0.9 maximum_bitcast_fusion
  94.1 2.3 %convolution_select_fusion = f32[2,4,8,9,256]{4,2,3,1,0:T(8,128)S(1)} fusion(bf16[3,3,3,256,256]{4,3,2,1,0:T(8,128)(2,1)S(1)} %bitcast.61, bf16[4,256,6,1,7,2]{1,4,5,2,0,3:T(8,128)(2,1)S(1)} %slice.144, bf16[4,256,6,1,8,9]{1,4,5,2,0,3:T(8,128)(2,1)S(1)} %copy.39, pred[8,9]{0,1:T(8,128)(4,1)S(1)} %copy-done), kind=kOutput, calls=%fused_computation.5 | convolution fusion | flops 2041823232 | bytes 5185608 | tf_op jit(solution)/shard_map/conv_general_dilated | solution.py:18
  97.1 0.6 squeeze.7
  97.9 12.0 %all_to_all.35 = bf16[2,16,16,256]{3,2,0,1:T(8,128)(2,1)S(1)} all-to-all(bf16[2,16,16,256]{3,2,0,1:T(8,128)(2,1)S(1)} %copy.43), channel_id=1, replica_groups=mesh['depth'=16,'filt'=16] {'filt'}, dimensions={1} | all-to-all | bytes 524288 | tf_op jit(solution)/shard_map/all_to_all | solution.py:89
  110.0 0.8 reshape.73
  (49 shorter events, 5.8 us)
Async XLA Ops:
  6.5 51.9 %all-gather.3.cloned.1.call-start = ((), (), s32[]{:S(2)}) async-start(), calls=%async_computation.3 | async-start | bytes 5640192 | tf_op jit(solution)/shard_map/all_gather | solution.py:50
  10.2 17.4 %collective-permute-start = (bf16[1,8,4096]{2,1,0:T(8,128)(2,1)S(1)}, bf16[1,8,4096]{2,1,0:T(8,128)(2,1)S(1)}, u32[]{:S(2)}, u32[]{:S(2)}) collective-permute-start(bf16[1,8,4096]{2,1,0:T(8,128)(2,1)S(1)} %get-tuple-element.25), channel_id=1, source_target_pairs={{0,16},{16,32},{32,48},{48,64},{64,80},{80,96},{96,112},{112,128},... | collective-permute-start | bytes 196616 | tf_op jit(solution)/shard_map/ppermute | solution.py:33
  13.8 13.8 %collective-permute-start.1 = (bf16[1,8,4096]{2,1,0:T(8,128)(2,1)S(1)}, bf16[1,8,4096]{2,1,0:T(8,128)(2,1)S(1)}, u32[]{:S(2)}, u32[]{:S(2)}) collective-permute-start(bf16[1,8,4096]{2,1,0:T(8,128)(2,1)S(1)} %get-tuple-element.26), channel_id=1, source_target_pairs={{16,0},{32,16},{48,32},{64,48},{80,64},{96,80},{112,96},{128,112},... | collective-permute-start | bytes 196616 | tf_op jit(solution)/shard_map/ppermute | solution.py:34
  20.7 20.4 %all-to-all-start.1 = ((f32[16,2,16]{2,1,0:T(2,128)}), f32[16,2,16]{2,1,0:T(2,128)S(1)}, u32[]{:S(2)}, u32[]{:S(2)}) async-start(f32[16,2,16]{2,1,0:T(2,128)} %broadcast_in_dim.4), calls=%async_computation.1 | async-start | bytes 32768 | tf_op jit(solution)/shard_map/all_to_all | solution.py:63
  41.1 15.7 %all-to-all-start = ((bf16[4,8,16,384]{3,1,0,2:T(8,128)(2,1)}), bf16[4,8,16,384]{3,1,0,2:T(8,128)(2,1)S(1)}, u32[]{:S(2)}, u32[]{:S(2)}) async-start(bf16[4,8,16,384]{3,1,0,2:T(8,128)(2,1)} %constant_dynamic-update-slice_fusion), calls=%async_computation | async-start | bytes 786432 | tf_op jit(solution)/shard_map/all_to_all | solution.py:81
  65.9 0.7 copy-start
  68.4 10.2 %collective-permute-start.2 = (bf16[1,256,4,64]{1,2,3,0:T(4,128)(2,1)S(1)}, bf16[1,256,4,64]{1,2,3,0:T(4,128)(2,1)S(1)}, u32[]{:S(2)}, u32[]{:S(2)}) collective-permute-start(bf16[1,256,4,64]{1,2,3,0:T(4,128)(2,1)S(1)} %get-tuple-element.23), channel_id=1, source_target_pairs={{0,16},{16,32},{32,48},{48,64},{64,80},{80,96},{96,112},{112,128},... | collective-permute-start | bytes 393224 | tf_op jit(solution)/shard_map/ppermute | solution.py:33
  72.0 7.4 %collective-permute-start.3 = (bf16[1,256,4,64]{1,2,3,0:T(4,128)(2,1)S(1)}, bf16[1,256,4,64]{1,2,3,0:T(4,128)(2,1)S(1)}, u32[]{:S(2)}, u32[]{:S(2)}) collective-permute-start(bf16[1,256,4,64]{1,2,3,0:T(4,128)(2,1)S(1)} %get-tuple-element.24), channel_id=1, source_target_pairs={{16,0},{32,16},{48,32},{64,48},{80,64},{96,80},{112,96},{128,112},... | collective-permute-start | bytes 393224 | tf_op jit(solution)/shard_map/ppermute | solution.py:34
  80.2 8.2 %collective-permute-start.4 = (bf16[4,256,1,64]{1,2,3,0:T(2,128)(2,1)S(1)}, bf16[4,256,1,64]{1,2,3,0:T(2,128)(2,1)S(1)}, u32[]{:S(2)}, u32[]{:S(2)}) collective-permute-start(bf16[4,256,1,64]{1,2,3,0:T(2,128)(2,1)S(1)} %get-tuple-element.5), channel_id=1, source_target_pairs={{0,1},{1,2},{2,3},{3,4},{4,5},{5,6},{6,7},{7,8},{8,9},{9,10},{10,1... | collective-permute-start | bytes 393224 | tf_op jit(solution)/shard_map/ppermute | solution.py:42
  84.8 2.4 %slice-start = ((bf16[16,165888]{1,0:T(8,128)(2,1)}), bf16[16,110592]{1,0:T(8,128)(2,1)S(1)}, s32[]{:S(2)}) async-start(bf16[16,165888]{1,0:T(8,128)(2,1)} %reshape.98), calls=%async_computation.4 | async-start | bytes 7077888 | tf_op jit(solution)/shard_map/slice | solution.py:53
  84.8 8.0 %collective-permute-start.5 = (bf16[4,256,1,64]{1,2,3,0:T(2,128)(2,1)S(1)}, bf16[4,256,1,64]{1,2,3,0:T(2,128)(2,1)S(1)}, u32[]{:S(2)}, u32[]{:S(2)}) collective-permute-start(bf16[4,256,1,64]{1,2,3,0:T(2,128)(2,1)S(1)} %get-tuple-element.6), channel_id=1, source_target_pairs={{1,0},{2,1},{3,2},{4,3},{5,4},{6,5},{7,6},{8,7},{9,8},{10,9},{11,1... | collective-permute-start | bytes 393224 | tf_op jit(solution)/shard_map/ppermute | solution.py:43
Sparse Core Ops, SparseCore 0:
  9.4 47.5 all-gather.2
where the time goes:
time: 119 us; the launch traced here: 118 us
  starting transfers between devices  37.6 us (32%)
  local copies, waits for them, and re-layouts  29.4 us (25%)
  waiting for transfers between devices  16.5 us (14%)
  between operations  13.7 us (12%)
  blocking collectives  12 us (10%)
  other arithmetic  4.87 us (4%)
  matrix products  3.57 us (3%)
    unnamed x22, local copies, waits for them, and re-layouts  13.7 us
    all_to_all x1, blocking collectives, local(): result = lax.all_to_all(second, 'filt', 1, 3, tiled=True)  12 us
    ppermute x2, starting transfers between devices, depth_halo(): high = lax.ppermute(block[:1], 'depth', backward)  10.9 us
    all_to_all x1, waiting for transfers between devices, local(): mine = lax.all_to_all(windows, 'filt', 2, 1, tiled=True)  9.9 us
    ppermute x2, starting transfers between devices, depth_halo(): low = lax.ppermute(block[block.shape[0] - 1:], 'depth', forward)  7.17 us
    all_to_all x1, starting transfers between devices, gather_biases(): whole = lax.all_to_all(spread, 'filt', 0, 0, tiled=True)  6.88 us
    all_to_all x1, starting transfers between devices, local(): mine = lax.all_to_all(windows, 'filt', 2, 1, tiled=True)  5.72 us
    all_gather x1, local copies, waits for them, and re-layouts, gather_kernels(): whole = lax.all_gather(flat, 'filt', axis=0, tiled=False)  5.6 us
  transfers between devices with their start and end apart: 9, of which 4 were waited for; matrix products, arithmetic and copies ran while one was open for 16% of the time, Pallas kernels for 0%

commit v1 on v0

--- a/solution.py
+++ b/solution.py
@@ -35,25 +35,35 @@
     return jnp.concatenate([low, block, high], axis=0)
 
 
-def row_halo(block):
-    count = lax.axis_size("filt")
-    forward = [(i, i + 1) for i in range(count - 1)]
-    backward = [(i + 1, i) for i in range(count - 1)]
-    above = lax.ppermute(block[:, :, block.shape[2] - 1 :], "filt", forward)
-    below = lax.ppermute(block[:, :, :1], "filt", backward)
-    return jnp.concatenate([above, block, below], axis=2)
+def full_halo(block):
+    depths, parts = lax.axis_size("depth"), lax.axis_size("filt")
+    last_plane, last_row = block.shape[0] - 1, block.shape[2] - 1
+
+    def moved(piece, step_d, step_f):
+        pairs = []
+        for d in range(depths):
+            for f in range(parts):
+                if 0 <= d + step_d < depths and 0 <= f + step_f < parts:
+                    pairs.append((d * parts + f, (d + step_d) * parts + f + step_f))
+        return lax.ppermute(piece, ("depth", "filt"), pairs)
+
+    top, bottom = block[last_plane:], block[:1]
+    above = moved(block[:, :, last_row:], 0, 1)
+    below = moved(block[:, :, :1], 0, -1)
+    low = jnp.concatenate(
+        [moved(top[:, :, last_row:], 1, 1), moved(top, 1, 0), moved(top[:, :, :1], 1, -1)], axis=2
+    )
+    high = jnp.concatenate(
+        [moved(bottom[:, :, last_row:], -1, 1), moved(bottom, -1, 0), moved(bottom[:, :, :1], -1, -1)], axis=2
+    )
+    middle = jnp.concatenate([above, block, below], axis=2)
+    return jnp.concatenate([low, middle, high], axis=0)
 
 
-def gather_kernels(first_kernel, second_kernel):
-    count = lax.axis_size("filt")
-    flat = jnp.concatenate([first_kernel.reshape(-1), second_kernel.reshape(-1)])
-    whole = lax.all_gather(flat, "filt", axis=0, tiled=False)
-    split = first_kernel.size
-    kernels = []
-    for part, kernel in ((whole[:, :split], first_kernel), (whole[:, split:], second_kernel)):
-        stacked = jnp.moveaxis(part.reshape((count,) + kernel.shape), 0, 3)
-        kernels.append(stacked.reshape(3, 3, 3, count * kernel.shape[3], kernel.shape[4]))
-    return kernels
+def flat_kernel(whole, kernel):
+    count = whole.shape[0]
+    stacked = jnp.moveaxis(whole.reshape((count,) + kernel.shape), 0, 3)
+    return stacked.reshape(3, 3, 3, count * kernel.shape[3], kernel.shape[4])
 
 
 def gather_biases(first_bias, second_bias):
@@ -69,20 +79,27 @@
     planes, chans, cells = features.shape
     rows = cells // SIDE
     block_rows = rows // count
-    kernel_1, kernel_2 = gather_kernels(first_kernel, second_kernel)
+    whole_2 = lax.all_gather(second_kernel.reshape(-1), "filt", axis=0, tiled=False)
     bias_1, bias_2 = gather_biases(first_bias, second_bias)
 
     extended = depth_halo(features).reshape(planes + 2, chans, rows, SIDE)
     framed = jnp.pad(extended, ((0, 0), (0, 0), (1, 1), (0, 0)))
-    windows = jnp.stack(
-        [framed[:, :, b * block_rows : b * block_rows + block_rows + 2] for b in range(count)], axis=2
-    )
-    windows = windows.reshape(planes + 2, chans, count, (block_rows + 2) * SIDE)
-    mine = lax.all_to_all(windows, "filt", 2, 1, tiled=True)
-    mine = mine.reshape(planes + 2, count * chans, block_rows + 2, SIDE)
+    blocks = framed[:, :, 1 : rows + 1].reshape(planes + 2, chans, count, block_rows, SIDE)
+    tops = framed[:, :, 0:rows:block_rows][:, :, :, None]
+    bottoms = framed[:, :, block_rows + 1 :: block_rows][:, :, :, None]
+    windows = jnp.concatenate([tops, blocks, bottoms], axis=3)
+    windows = jnp.moveaxis(windows, 2, 0).reshape(count, -1)
+    shard_1 = jnp.broadcast_to(first_kernel.reshape(1, -1), (count, first_kernel.size))
+    sent = jnp.concatenate([windows, shard_1], axis=1)
+    got = lax.all_to_all(sent, "filt", 0, 0, tiled=True)
+    split = windows.shape[1]
+    mine = got[:, :split].reshape(count, planes + 2, chans, block_rows + 2, SIDE)
+    mine = jnp.moveaxis(mine, 0, 1).reshape(planes + 2, count * chans, block_rows + 2, SIDE)
+    kernel_1 = flat_kernel(got[:, split:], first_kernel)
 
     hidden = activate(conv(mine, kernel_1), bias_1)
-    second = activate(conv(row_halo(depth_halo(hidden)), kernel_2), bias_2)
+    kernel_2 = flat_kernel(whole_2, second_kernel)
+    second = activate(conv(full_halo(hidden), kernel_2), bias_2)
 
     outs = second_kernel.shape[3]
     second = second.reshape(planes, count, outs, block_rows * SIDE)

time: 119 us -> 241 us (2.03)
  other arithmetic: 4.87 us -> 80.1 us
  waiting for transfers between devices: 16.5 us -> 45.9 us
  starting transfers between devices: 37.6 us -> 48.4 us
  local copies, waits for them, and re-layouts: 29.4 us -> 33.8 us
    all_gather x0 -> x1, other arithmetic: none -> 74 us  [local(): lax.all_gather(second_kernel.reshape(-1), 'filt', axis=0, tiled=False)]
    all_to_all x1, waiting for transfers between devices: 9.9 us -> 36.9 us  [local(): got = lax.all_to_all(sent, 'filt', 0, 0, tiled=True)]
    ppermute x2 -> x8, starting transfers between devices: 6.94 us -> 26.6 us  [moved(): return lax.ppermute(piece, ('depth', 'filt'), pairs)]
    unnamed x22 -> x18, local copies, waits for them, and re-layouts: 13.7 us -> 19.9 us
    all_gather x1 -> x0, local copies, waits for them, and re-layouts: 5.6 us -> none  [gather_kernels(): whole = lax.all_gather(flat, 'filt', axis=0, tiled=False)]
    ppermute x2 -> x1, starting transfers between devices: 10.9 us -> 5.63 us  [depth_halo(): high = lax.ppermute(block[:1], 'depth', backward)]
    ppermute x2 -> x8, waiting for transfers between devices: 4.38 us -> 8.99 us  [moved(): return lax.ppermute(piece, ('depth', 'filt'), pairs)]
    ppermute x2 -> x1, starting transfers between devices: 7.17 us -> 3.55 us  [depth_halo(): low = lax.ppermute(block[block.shape[0] - 1:], 'depth', forward)]
  transfers between devices with their start and end apart: 9 -> 13, of which waited for: 4 -> 3; matrix products, arithmetic and copies ran while one was open for 16% -> 15% of each run, Pallas kernels for 0% -> 0%
where the time goes in v1:
time: 241 us; the launch traced here: 240 us
  other arithmetic  80.1 us (33%)
  starting transfers between devices  48.4 us (20%)
  waiting for transfers between devices  45.9 us (19%)
  local copies, waits for them, and re-layouts  33.8 us (14%)
  between operations  13.9 us (6%)
  blocking collectives  13 us (5%)
  matrix products  5.03 us (2%)
    all_gather x1, other arithmetic, local(): lax.all_gather(second_kernel.reshape(-1), 'filt', axis=0, tiled=False)  74 us
    all_to_all x1, waiting for transfers between devices, local(): got = lax.all_to_all(sent, 'filt', 0, 0, tiled=True)  36.9 us
    ppermute x8, starting transfers between devices, moved(): return lax.ppermute(piece, ('depth', 'filt'), pairs)  26.6 us
    unnamed x18, local copies, waits for them, and re-layouts  19.9 us
    all_to_all x1, blocking collectives, local(): result = lax.all_to_all(second, 'filt', 1, 3, tiled=True)  13 us
    ppermute x8, waiting for transfers between devices, moved(): return lax.ppermute(piece, ('depth', 'filt'), pairs)  8.99 us
    all_to_all x1, starting transfers between devices, gather_biases(): whole = lax.all_to_all(spread, 'filt', 0, 0, tiled=True)  6.88 us
    all_to_all x1, starting transfers between devices, local(): got = lax.all_to_all(sent, 'filt', 0, 0, tiled=True)  5.71 us
  transfers between devices with their start and end apart: 13, of which 3 were waited for; matrix products, arithmetic and copies ran while one was open for 15% of the time, Pallas kernels for 0%

profile of v1, /device:TPU:17, one launch (start us, length us, event | category | flops | bytes accessed | tf_op | source)
XLA Modules:
  0.0 240.1 jit_solution(5924272607682375881)
XLA Ops:
  6.5 1.8 reshape.73
  8.3 0.9 fusion.28
  9.2 3.5 %collective-permute-start = (bf16[1,8,4096]{2,1,0:T(8,128)(2,1)S(1)}, bf16[1,8,4096]{2,1,0:T(8,128)(2,1)S(1)}, u32[]{:S(2)}, u32[]{:S(2)}) collective-permute-start(bf16[1,8,4096]{2,1,0:T(8,128)(2,1)S(1)} %get-tuple-element.14), channel_id=1, source_target_pairs={{0,16},{16,32},{32,48},{48,64},{64,80},{80,96},{96,112},{112,128},... | collective-permute-start | bytes 196616 | tf_op jit(solution)/shard_map/ppermute | solution.py:33
  12.8 5.6 %collective-permute-start.1 = (bf16[1,8,4096]{2,1,0:T(8,128)(2,1)S(1)}, bf16[1,8,4096]{2,1,0:T(8,128)(2,1)S(1)}, u32[]{:S(2)}, u32[]{:S(2)}) collective-permute-start(bf16[1,8,4096]{2,1,0:T(8,128)(2,1)S(1)} %get-tuple-element.13), channel_id=1, source_target_pairs={{16,0},{32,16},{48,32},{64,48},{80,64},{96,80},{112,96},{128,112},... | collective-permute-start | bytes 196616 | tf_op jit(solution)/shard_map/ppermute | solution.py:34
  18.4 0.7 pad_maximum_fusion
  19.1 0.6 broadcast_in_dim.26
  19.7 6.9 %all-to-all-start.1 = ((f32[16,2,16]{2,1,0:T(2,128)}), f32[16,2,16]{2,1,0:T(2,128)S(1)}, u32[]{:S(2)}, u32[]{:S(2)}) async-start(f32[16,2,16]{2,1,0:T(2,128)} %broadcast_in_dim.26), calls=%async_computation.1 | async-start | bytes 32768 | tf_op jit(solution)/shard_map/all_to_all | solution.py:73
  26.6 0.9 pad.25.clone
  27.5 0.9 constant_dynamic-update-slice_fusion.1
  28.5 0.5 reshape.40
  29.2 0.3 slice.56
  29.5 0.3 slice.55
  29.8 0.5 reshape.41
  30.8 1.1 maximum_bitcast_fusion.1
  31.9 0.8 reshape.42
  33.0 0.5 broadcast.58
  33.5 2.9 %reduce.5 = bf16[16,67584]{1,0:T(8,128)(2,1)} reduce(bf16[16,1,67584]{2,0,1:T(8,128)(2,1)S(1)} %maximum_bitcast_fusion, bf16[]{:T(256)} %broadcast.58), dimensions={1}, to_apply=%copy.60.reduce_sub_computation | reduce | bytes 4325378 | tf_op jit(solution)/shard_map/all_to_all | solution.py:94
  36.4 4.1 %reshape.86 = bf16[16,2,33792]{2,1,0:T(2,128)(2,1)} reshape(bf16[16,67584]{1,0:T(8,128)(2,1)} %reduce.5) | data formatting | bytes 4325376
  40.5 5.7 %all-to-all-start = ((bf16[16,2,33792]{2,1,0:T(2,128)(2,1)}), bf16[16,2,33792]{2,1,0:T(2,128)(2,1)S(1)}, u32[]{:S(2)}, u32[]{:S(2)}) async-start(bf16[16,2,33792]{2,1,0:T(2,128)(2,1)} %reshape.86), calls=%async_computation | async-start | bytes 4325376 | tf_op jit(solution)/shard_map/all_to_all | solution.py:94
  46.3 36.9 %all-to-all-done = bf16[16,2,33792]{2,1,0:T(2,128)(2,1)S(1)} async-done(((bf16[16,2,33792]{2,1,0:T(2,128)(2,1)}), bf16[16,2,33792]{2,1,0:T(2,128)(2,1)S(1)}, u32[]{:S(2)}, u32[]{:S(2)}) %all-to-all-start) | async-done | bytes 2162720 | tf_op jit(solution)/shard_map/all_to_all | solution.py:94
  83.3 6.6 %reshape.87 = bf16[16,1,67584]{2,1,0:T(2,128)(2,1)} reshape(bf16[16,2,33792]{2,1,0:T(2,128)(2,1)S(1)} %all-to-all-done) | data formatting | bytes 4325376
  89.9 3.5 %copy.85 = bf16[16,1,67584]{2,0,1:T(8,128)(2,1)S(1)} copy(bf16[16,1,67584]{2,1,0:T(2,128)(2,1)} %reshape.87) | data formatting | bytes 4325376
  93.7 1.8 copy.65
  95.5 0.9 reshape.43
  96.6 0.3 copy.78
  97.3 2.7 %convolution_select_fusion.1 = f32[2,4,8,9,256]{4,2,3,1,0:T(8,128)S(1)} fusion(bf16[3,3,3,256,128]{4,3,2,1,0:T(8,128)(2,1)} %bitcast.74, bf16[4,128,6,1,7,2]{1,4,5,2,0,3:T(8,128)(2,1)S(1)} %slice.74, bf16[4,128,6,1,8,9]{1,4,5,2,0,3:T(8,128)(2,1)S(1)} %copy.64, pred[8,9]{0,1:T(8,128)(4,1)S(1)} %copy-done.3), kind=kOutput, calls=%fused_computation.8 | convolution fusion | flops 1020985344 | bytes 2887752 | tf_op jit(solution)/shard_map/conv_general_dilated | solution.py:18
  100.6 5.1 %collective-permute-start.9 = (bf16[1,256,1,64]{1,2,3,0:T(2,128)(2,1)S(1)}, bf16[1,256,1,64]{1,2,3,0:T(2,128)(2,1)S(1)}, u32[]{:S(2)}, u32[]{:S(2)}) collective-permute-start(bf16[1,256,1,64]{1,2,3,0:T(2,128)(2,1)S(1)} %get-tuple-element.6), channel_id=1, source_target_pairs={{17,0},{18,1},{19,2},{20,3},{21,4},{22,5},{23,6},{24,7},{25,8},{26... | collective-permute-start | bytes 98312 | tf_op jit(solution)/shard_map/ppermute | solution.py:48
  105.9 2.8 %collective-permute-start.8 = (bf16[1,256,4,64]{1,2,3,0:T(4,128)(2,1)S(1)}, bf16[1,256,4,64]{1,2,3,0:T(4,128)(2,1)S(1)}, u32[]{:S(2)}, u32[]{:S(2)}) collective-permute-start(bf16[1,256,4,64]{1,2,3,0:T(4,128)(2,1)S(1)} %get-tuple-element.10), channel_id=1, source_target_pairs={{16,0},{17,1},{18,2},{19,3},{20,4},{21,5},{22,6},{23,7},{24,8},{25... | collective-permute-start | bytes 393224 | tf_op jit(solution)/shard_map/ppermute | solution.py:48
  108.7 5.1 %collective-permute-start.7 = (bf16[1,256,1,64]{1,2,3,0:T(2,128)(2,1)S(1)}, bf16[1,256,1,64]{1,2,3,0:T(2,128)(2,1)S(1)}, u32[]{:S(2)}, u32[]{:S(2)}) collective-permute-start(bf16[1,256,1,64]{1,2,3,0:T(2,128)(2,1)S(1)} %get-tuple-element.7), channel_id=1, source_target_pairs={{16,1},{17,2},{18,3},{19,4},{20,5},{21,6},{22,7},{23,8},{24,9},{25... | collective-permute-start | bytes 98312 | tf_op jit(solution)/shard_map/ppermute | solution.py:48
  113.8 4.0 %collective-permute-start.3 = (bf16[1,256,4,64]{1,2,3,0:T(4,128)(2,1)S(1)}, bf16[1,256,4,64]{1,2,3,0:T(4,128)(2,1)S(1)}, u32[]{:S(2)}, u32[]{:S(2)}) collective-permute-start(bf16[1,256,4,64]{1,2,3,0:T(4,128)(2,1)S(1)} %get-tuple-element.9), channel_id=1, source_target_pairs={{0,16},{1,17},{2,18},{3,19},{4,20},{5,21},{6,22},{7,23},{8,24},{9,... | collective-permute-start | bytes 393224 | tf_op jit(solution)/shard_map/ppermute | solution.py:48
  118.0 1.9 collective-permute-start.4
  119.9 1.9 collective-permute-start.6
  121.8 3.6 %collective-permute-start.5 = (bf16[2,256,1,64]{1,2,3,0:T(2,128)(2,1)S(1)}, bf16[2,256,1,64]{1,2,3,0:T(2,128)(2,1)S(1)}, u32[]{:S(2)}, u32[]{:S(2)}) collective-permute-start(bf16[2,256,1,64]{1,2,3,0:T(2,128)(2,1)S(1)} %get-tuple-element.11), channel_id=1, source_target_pairs={{0,1},{1,2},{2,3},{3,4},{4,5},{5,6},{6,7},{7,8},{8,9},{9,10},{10,1... | collective-permute-start | bytes 196616 | tf_op jit(solution)/shard_map/ppermute | solution.py:48
  125.5 1.9 collective-permute-done.4
  127.4 2.1 collective-permute-start.2
  129.6 7.0 %collective-permute-done.2 = bf16[1,256,1,64]{1,2,3,0:T(2,128)(2,1)S(1)} collective-permute-done((bf16[1,256,1,64]{1,2,3,0:T(2,128)(2,1)S(1)}, bf16[1,256,1,64]{1,2,3,0:T(2,128)(2,1)S(1)}, u32[]{:S(2)}, u32[]{:S(2)}) %collective-permute-start.2) | collective-permute-done | bytes 32800 | tf_op jit(solution)/shard_map/ppermute | solution.py:48
  136.6 0.9 maximum_bitcast_fusion.2
  137.9 0.9 copy-done
  138.8 0.7 slice.86
  139.5 74.0 %reduce.1 = bf16[16,110592]{1,0:T(8,128)(2,1)S(1)} reduce(bf16[16,1,110592]{2,1,0:T(2,128)(2,1)} %all-gather.3.cloned.1.call-done, bf16[]{:T(256)} %constant.21), dimensions={1}, to_apply=%all-gather.reduce_sub_computation | reduce | bytes 7077890 | tf_op jit(solution)/shard_map/all_gather | solution.py:82
  213.6 0.7 copy.80
  214.3 0.4 copy.70
  214.8 0.7 copy-done.1
  215.5 2.3 convolution_select_fusion
  218.1 0.4 copy.72
  218.5 0.6 squeeze.7
  219.3 13.0 %all_to_all.32 = bf16[2,16,16,256]{3,2,0,1:T(8,128)(2,1)S(1)} all-to-all(bf16[2,16,16,256]{3,2,0,1:T(8,128)(2,1)S(1)} %copy.73), channel_id=1, replica_groups=mesh['depth'=16,'filt'=16] {'filt'}, dimensions={1} | all-to-all | bytes 524288 | tf_op jit(solution)/shard_map/all_to_all | solution.py:106
  232.4 0.8 reshape.48
  (45 shorter events, 3.7 us)
Async XLA Ops:
  6.5 133.0 %all-gather.3.cloned.1.call-start = ((), (), s32[]{:S(2)}) async-start(), calls=%async_computation.3 | async-start | bytes 7520256 | tf_op jit(solution)/shard_map/all_gather | solution.py:82
  9.2 18.3 %collective-permute-start = (bf16[1,8,4096]{2,1,0:T(8,128)(2,1)S(1)}, bf16[1,8,4096]{2,1,0:T(8,128)(2,1)S(1)}, u32[]{:S(2)}, u32[]{:S(2)}) collective-permute-start(bf16[1,8,4096]{2,1,0:T(8,128)(2,1)S(1)} %get-tuple-element.14), channel_id=1, source_target_pairs={{0,16},{16,32},{32,48},{48,64},{64,80},{80,96},{96,112},{112,128},... | collective-permute-start | bytes 196616 | tf_op jit(solution)/shard_map/ppermute | solution.py:33
  12.8 15.7 %collective-permute-start.1 = (bf16[1,8,4096]{2,1,0:T(8,128)(2,1)S(1)}, bf16[1,8,4096]{2,1,0:T(8,128)(2,1)S(1)}, u32[]{:S(2)}, u32[]{:S(2)}) collective-permute-start(bf16[1,8,4096]{2,1,0:T(8,128)(2,1)S(1)} %get-tuple-element.13), channel_id=1, source_target_pairs={{16,0},{32,16},{48,32},{64,48},{80,64},{96,80},{112,96},{128,112},... | collective-permute-start | bytes 196616 | tf_op jit(solution)/shard_map/ppermute | solution.py:34
  19.7 20.8 %all-to-all-start.1 = ((f32[16,2,16]{2,1,0:T(2,128)}), f32[16,2,16]{2,1,0:T(2,128)S(1)}, u32[]{:S(2)}, u32[]{:S(2)}) async-start(f32[16,2,16]{2,1,0:T(2,128)} %broadcast_in_dim.26), calls=%async_computation.1 | async-start | bytes 32768 | tf_op jit(solution)/shard_map/all_to_all | solution.py:73
  40.5 42.7 %all-to-all-start = ((bf16[16,2,33792]{2,1,0:T(2,128)(2,1)}), bf16[16,2,33792]{2,1,0:T(2,128)(2,1)S(1)}, u32[]{:S(2)}, u32[]{:S(2)}) async-start(bf16[16,2,33792]{2,1,0:T(2,128)(2,1)} %reshape.86), calls=%async_computation | async-start | bytes 4325376 | tf_op jit(solution)/shard_map/all_to_all | solution.py:94
  96.5 0.8 copy-start.3
  100.6 19.3 %collective-permute-start.9 = (bf16[1,256,1,64]{1,2,3,0:T(2,128)(2,1)S(1)}, bf16[1,256,1,64]{1,2,3,0:T(2,128)(2,1)S(1)}, u32[]{:S(2)}, u32[]{:S(2)}) collective-permute-start(bf16[1,256,1,64]{1,2,3,0:T(2,128)(2,1)S(1)} %get-tuple-element.6), channel_id=1, source_target_pairs={{17,0},{18,1},{19,2},{20,3},{21,4},{22,5},{23,6},{24,7},{25,8},{26... | collective-permute-start | bytes 98312 | tf_op jit(solution)/shard_map/ppermute | solution.py:48
  105.9 30.7 %collective-permute-start.8 = (bf16[1,256,4,64]{1,2,3,0:T(4,128)(2,1)S(1)}, bf16[1,256,4,64]{1,2,3,0:T(4,128)(2,1)S(1)}, u32[]{:S(2)}, u32[]{:S(2)}) collective-permute-start(bf16[1,256,4,64]{1,2,3,0:T(4,128)(2,1)S(1)} %get-tuple-element.10), channel_id=1, source_target_pairs={{16,0},{17,1},{18,2},{19,3},{20,4},{21,5},{22,6},{23,7},{24,8},{25... | collective-permute-start | bytes 393224 | tf_op jit(solution)/shard_map/ppermute | solution.py:48
  108.7 13.2 %collective-permute-start.7 = (bf16[1,256,1,64]{1,2,3,0:T(2,128)(2,1)S(1)}, bf16[1,256,1,64]{1,2,3,0:T(2,128)(2,1)S(1)}, u32[]{:S(2)}, u32[]{:S(2)}) collective-permute-start(bf16[1,256,1,64]{1,2,3,0:T(2,128)(2,1)S(1)} %get-tuple-element.7), channel_id=1, source_target_pairs={{16,1},{17,2},{18,3},{19,4},{20,5},{21,6},{22,7},{23,8},{24,9},{25... | collective-permute-start | bytes 98312 | tf_op jit(solution)/shard_map/ppermute | solution.py:48
  113.8 22.8 %collective-permute-start.3 = (bf16[1,256,4,64]{1,2,3,0:T(4,128)(2,1)S(1)}, bf16[1,256,4,64]{1,2,3,0:T(4,128)(2,1)S(1)}, u32[]{:S(2)}, u32[]{:S(2)}) collective-permute-start(bf16[1,256,4,64]{1,2,3,0:T(4,128)(2,1)S(1)} %get-tuple-element.9), channel_id=1, source_target_pairs={{0,16},{1,17},{2,18},{3,19},{4,20},{5,21},{6,22},{7,23},{8,24},{9,... | collective-permute-start | bytes 393224 | tf_op jit(solution)/shard_map/ppermute | solution.py:48
  118.0 9.4 %collective-permute-start.4 = (bf16[1,256,1,64]{1,2,3,0:T(2,128)(2,1)S(1)}, bf16[1,256,1,64]{1,2,3,0:T(2,128)(2,1)S(1)}, u32[]{:S(2)}, u32[]{:S(2)}) collective-permute-start(bf16[1,256,1,64]{1,2,3,0:T(2,128)(2,1)S(1)} %get-tuple-element.8), channel_id=1, source_target_pairs={{1,16},{2,17},{3,18},{4,19},{5,20},{6,21},{7,22},{8,23},{9,24},{10... | collective-permute-start | bytes 98312 | tf_op jit(solution)/shard_map/ppermute | solution.py:48
  119.9 16.7 %collective-permute-start.6 = (bf16[2,256,1,64]{1,2,3,0:T(2,128)(2,1)S(1)}, bf16[2,256,1,64]{1,2,3,0:T(2,128)(2,1)S(1)}, u32[]{:S(2)}, u32[]{:S(2)}) collective-permute-start(bf16[2,256,1,64]{1,2,3,0:T(2,128)(2,1)S(1)} %get-tuple-element.12), channel_id=1, source_target_pairs={{1,0},{2,1},{3,2},{4,3},{5,4},{6,5},{7,6},{8,7},{9,8},{10,9},{11,1... | collective-permute-start | bytes 196616 | tf_op jit(solution)/shard_map/ppermute | solution.py:48
  121.8 14.8 %collective-permute-start.5 = (bf16[2,256,1,64]{1,2,3,0:T(2,128)(2,1)S(1)}, bf16[2,256,1,64]{1,2,3,0:T(2,128)(2,1)S(1)}, u32[]{:S(2)}, u32[]{:S(2)}) collective-permute-start(bf16[2,256,1,64]{1,2,3,0:T(2,128)(2,1)S(1)} %get-tuple-element.11), channel_id=1, source_target_pairs={{0,1},{1,2},{2,3},{3,4},{4,5},{5,6},{6,7},{7,8},{8,9},{9,10},{10,1... | collective-permute-start | bytes 196616 | tf_op jit(solution)/shard_map/ppermute | solution.py:48
  127.4 9.2 %collective-permute-start.2 = (bf16[1,256,1,64]{1,2,3,0:T(2,128)(2,1)S(1)}, bf16[1,256,1,64]{1,2,3,0:T(2,128)(2,1)S(1)}, u32[]{:S(2)}, u32[]{:S(2)}) collective-permute-start(bf16[1,256,1,64]{1,2,3,0:T(2,128)(2,1)S(1)} %get-tuple-element.5), channel_id=1, source_target_pairs={{0,17},{1,18},{2,19},{3,20},{4,21},{5,22},{6,23},{7,24},{8,25},{9,... | collective-permute-start | bytes 98312 | tf_op jit(solution)/shard_map/ppermute | solution.py:48
  137.9 0.9 copy-start
  214.3 1.2 copy-start.1
  214.3 1.2 copy-start.2
Sparse Core Ops, SparseCore 0:
  9.2 74.7 all-gather.2

commit v2 on v0

v2 whole, which is shorter than its diff:
```python
import jax
import jax.numpy as jnp
from jax import lax
from jax.sharding import PartitionSpec as P

SIDE = 64


leak_slope = 0.3


def activate(summed, bias):
    shifted = summed + bias[None, :, None, None]
    return jnp.where(shifted > 0, shifted, leak_slope * shifted).astype(jnp.bfloat16)


def conv(framed, kernel):
    summed = lax.conv_general_dilated(
        framed[None],
        kernel,
        (1, 1, 1),
        ((0, 0), (0, 0), (1, 1)),
        dimension_numbers=("NDCHW", "ODHWI", "NDCHW"),
        preferred_element_type=jnp.float32,
    )
    return summed[0]


def depth_halo(block, reach):
    count = lax.axis_size("depth")
    forward = [(i, i + 1) for i in range(count - 1)]
    backward = [(i + 1, i) for i in range(count - 1)]
    low = lax.ppermute(block[block.shape[0] - reach :], "depth", forward)
    high = lax.ppermute(block[:reach], "depth", backward)
    return jnp.concatenate([low, block, high], axis=0)


def gather_kernels(first_kernel, second_kernel):
    outs, chans = first_kernel.shape[3], first_kernel.shape[4]
    first = jnp.moveaxis(first_kernel.reshape(27, outs, chans), 1, 0)
    second = jnp.moveaxis(second_kernel.reshape(27, outs, second_kernel.shape[4]), 1, 0)
    whole = lax.all_gather(jnp.concatenate([first, second], axis=2), "filt", axis=0, tiled=True)
    total = whole.shape[0]
    return (
        whole[:, :, :chans].reshape(total, 3, 3, 3, chans),
        whole[:, :, chans:].reshape(total, 3, 3, 3, second_kernel.shape[4]),
    )


def gather_biases(first_bias, second_bias):
    count = lax.axis_size("filt")
    pair = jnp.stack([first_bias, second_bias])
    spread = jnp.broadcast_to(pair[None], (count,) + pair.shape)
    whole = lax.all_to_all(spread, "filt", 0, 0, tiled=True)
    return whole[:, 0].reshape(-1), whole[:, 1].reshape(-1)


def inside(count_planes, count_rows, planes, block_rows):
    plane = lax.axis_index("depth") * planes - 1 + jnp.arange(planes + 2)
    row = lax.axis_index("filt") * block_rows - 1 + jnp.arange(block_rows + 2)
    plane_ok = (plane >= 0) & (plane < count_planes)
    row_ok = (row >= 0) & (row < count_rows)
    return plane_ok[:, None, None, None] & row_ok[None, None, :, None]


def local(features, first_kernel, first_bias, second_kernel, second_bias):
    count = lax.axis_size("filt")
    planes, chans, cells = features.shape
    rows = cells // SIDE
    block_rows = rows // count
    kernel_1, kernel_2 = gather_kernels(first_kernel, second_kernel)
    bias_1, bias_2 = gather_biases(first_bias, second_bias)

    extended = depth_halo(features, 2).reshape(planes + 4, chans, rows, SIDE)
    framed = jnp.pad(extended, ((0, 0), (0, 0), (2, max(2, block_rows)), (0, 0)))
    heads = framed[:, :, :rows].reshape(planes + 4, chans, count, block_rows, SIDE)
    tails = framed[:, :, block_rows : rows + block_rows].reshape(planes + 4, chans, count, block_rows, SIDE)
    windows = jnp.concatenate([heads, tails[:, :, :, : 4]], axis=3)
    windows = windows.reshape(planes + 4, chans, count, (block_rows + 4) * SIDE)
    mine = lax.all_to_all(windows, "filt", 2, 1, tiled=True)
    mine = mine.reshape(planes + 4, count * chans, block_rows + 4, SIDE)

    hidden = activate(conv(mine, kernel_1), bias_1)
    grid = inside(planes * lax.axis_size("depth"), rows, planes, block_rows)
    hidden = jnp.where(grid, hidden, jnp.zeros_like(hidden))
    second = activate(conv(hidden, kernel_2), bias_2)

    outs = second_kernel.shape[3]
    second = second.reshape(planes, count, outs, block_rows * SIDE)
    result = lax.all_to_all(second, "filt", 1, 3, tiled=True)
    return result.reshape(planes, outs, cells)


def solution(mesh):
    in_specs = (
        P("depth", "filt", None),
        P(None, None, None, "filt", None),
        P("filt"),
        P(None, None, None, "filt", None),
        P("filt"),
    )
    out_specs = P("depth", "filt", None)
    return jax.shard_map(local, mesh=mesh, in_specs=in_specs, out_specs=out_specs, check_vma=False)
```

time: 119 us -> 94.1 us (0.79)
  local copies, waits for them, and re-layouts: 29.4 us -> 13.4 us
  starting transfers between devices: 37.6 us -> 21.8 us
  waiting for transfers between devices: 16.5 us -> 22.3 us
  matrix products: 3.57 us -> 6.06 us
    ppermute x6 -> x2, starting transfers between devices: 25 us -> 9.18 us  [the longest x1 5.63 us: depth_halo(): high = lax.ppermute(block[:reach], 'depth', backward)]
    unnamed x22 -> x3, local copies, waits for them, and re-layouts: 13.7 us -> 1.12 us
    all_to_all x1, waiting for transfers between devices: 9.9 us -> 18.9 us  [local(): mine = lax.all_to_all(windows, 'filt', 2, 1, tiled=True)]
    ppermute x6 -> x2, waiting for transfers between devices: 6.53 us -> 0.01 us  [the longest x1 0.01 us: depth_halo(): low = lax.ppermute(block[block.shape[0] - reach:], 'depth', forward)]
    all_gather x1 -> x0, local copies, waits for them, and re-layouts: 5.6 us -> none  [gather_kernels(): whole = lax.all_gather(flat, 'filt', axis=0, tiled=False)]
    slice x6 -> x7, local copies, waits for them, and re-layouts: 1.71 us -> 5.16 us  [the longest x2 1.99 us: gather_kernels(): whole[:, :, chans:].reshape(total, 3, 3, 3, second_kernel.shape[4])]
    all_gather x1, waiting for transfers between devices: 0.02 us -> 3.42 us  [gather_kernels(): lax.all_gather(jnp.concatenate([first, second], axis=2), 'filt', axis=0,...]
    another operation x17 -> x0, local copies, waits for them, and re-layouts: 2.49 us -> none  [local(): jnp.stack([framed[:, :, b * block_rows:b * block_rows + block_rows + 2] f...]
  transfers between devices with their start and end apart: 9 -> 5, of which waited for: 4 -> 2; matrix products, arithmetic and copies ran while one was open for 16% -> 10% of each run, Pallas kernels for 0% -> 0%
where the time goes in v2:
time: 94.1 us; the launch traced here: 92.4 us
  waiting for transfers between devices  22.3 us (24%)
  starting transfers between devices  21.8 us (23%)
  between operations  13.6 us (14%)
  local copies, waits for them, and re-layouts  13.4 us (14%)
  blocking collectives  11.2 us (12%)
  matrix products  6.06 us (6%)
  other arithmetic  3.95 us (4%)
    all_to_all x1, waiting for transfers between devices, local(): mine = lax.all_to_all(windows, 'filt', 2, 1, tiled=True)  18.9 us
    all_to_all x1, blocking collectives, local(): result = lax.all_to_all(second, 'filt', 1, 3, tiled=True)  11.2 us
    all_to_all x1, starting transfers between devices, gather_biases(): whole = lax.all_to_all(spread, 'filt', 0, 0, tiled=True)  6.88 us
    conv_general_dilated x2, matrix products, conv(): lax.conv_general_dilated(framed[None], kernel, (1, 1, 1), ((0, 0), (0, 0)...  6.06 us
    all_to_all x1, starting transfers between devices, local(): mine = lax.all_to_all(windows, 'filt', 2, 1, tiled=True)  5.72 us
    ppermute x1, starting transfers between devices, depth_halo(): high = lax.ppermute(block[:reach], 'depth', backward)  5.63 us
    ppermute x1, starting transfers between devices, depth_halo(): low = lax.ppermute(block[block.shape[0] - reach:], 'depth', forward)  3.55 us
    all_gather x1, waiting for transfers between devices, gather_kernels(): lax.all_gather(jnp.concatenate([first, second], axis=2), 'filt', axis=0,...  3.42 us
  transfers between devices with their start and end apart: 5, of which 2 were waited for; matrix products, arithmetic and copies ran while one was open for 10% of the time, Pallas kernels for 0%

profile of v2, /device:TPU:17, one launch (start us, length us, event | category | flops | bytes accessed | tf_op | source)
XLA Modules:
  0.0 92.4 jit_solution(1947402109707797569)
XLA Ops:
  6.5 0.0 all-gather.2.cloned.1.call-start
  6.5 1.8 %pad_maximum_fusion.2 = bf16[16,27,384]{2,0,1:T(8,128)(2,1)} fusion(bf16[16,27,256]{2,0,1:T(8,128)(2,1)} %bitcast.53, bf16[16,27,128]{2,0,1:T(8,128)(2,1)} %bitcast.54), kind=kLoop, calls=%fused_computation.34 | loop fusion | flops 663552 | bytes 663552 | tf_op jit(solution)/shard_map/concatenate | solution.py:42
  8.3 0.0 all-gather.2.cloned.1.call-update
  8.3 3.5 %collective-permute-start = (bf16[2,8,4096]{2,1,0:T(8,128)(2,1)}, bf16[2,8,4096]{2,1,0:T(8,128)(2,1)S(1)}, u32[]{:S(2)}, u32[]{:S(2)}) collective-permute-start(bf16[2,8,4096]{2,1,0:T(8,128)(2,1)} %param.5), channel_id=1, source_target_pairs={{0,16},{16,32},{32,48},{48,64},{64,80},{80,96},{96,112},{112,128},... | collective-permute-start | bytes 393224 | tf_op jit(solution)/shard_map/ppermute | solution.py:33
  11.9 5.6 %collective-permute-start.1 = (bf16[2,8,4096]{2,1,0:T(8,128)(2,1)}, bf16[2,8,4096]{2,1,0:T(8,128)(2,1)S(1)}, u32[]{:S(2)}, u32[]{:S(2)}) collective-permute-start(bf16[2,8,4096]{2,1,0:T(8,128)(2,1)} %param.5), channel_id=1, source_target_pairs={{16,0},{32,16},{48,32},{64,48},{80,64},{96,80},{112,96},{128,112},... | collective-permute-start | bytes 393224 | tf_op jit(solution)/shard_map/ppermute | solution.py:34
  17.5 0.7 pad_maximum_fusion.3
  18.2 0.6 broadcast_in_dim.13
  18.8 6.9 %all-to-all-start.1 = ((f32[16,2,16]{2,1,0:T(2,128)}), f32[16,2,16]{2,1,0:T(2,128)S(1)}, u32[]{:S(2)}, u32[]{:S(2)}) async-start(f32[16,2,16]{2,1,0:T(2,128)} %broadcast_in_dim.13), calls=%async_computation.1 | async-start | bytes 32768 | tf_op jit(solution)/shard_map/all_to_all | solution.py:54
  25.7 0.0 collective-permute-done
  25.7 0.0 collective-permute-done.1
  25.7 1.0 %pad_maximum_fusion.1 = bf16[6,8,4096]{2,1,0:T(8,128)(2,1)S(1)} fusion(bf16[2,8,4096]{2,1,0:T(8,128)(2,1)S(1)} %collective-permute-done.1, bf16[2,8,4096]{2,1,0:T(8,128)(2,1)} %param.5, bf16[2,8,4096]{2,1,0:T(8,128)(2,1)S(1)} %collective-permute-done), kind=kLoop, calls=%fused_computation.33 | loop fusion | flops 393216 | bytes 786432 | tf_op jit(solution)/shard_map/concatenate | solution.py:35
  26.7 0.8 reshape.83
  27.5 0.7 pad_slice_fusion.1
  28.2 0.5 copy.37
  28.7 0.5 copy.38
  29.3 0.3 pad_maximum_fusion
  29.6 0.5 copy.49
  30.0 1.7 %reshape.107 = bf16[6,8,16,512]{3,1,0,2:T(8,128)(2,1)} reshape(bf16[6,8,16,8,64]{4,3,1,0,2:T(8,128)(2,1)S(1)} %copy.49) | data formatting | bytes 1572864 | tf_op jit(solution)/shard_map/reshape | solution.py:79
  31.7 0.0 all-to-all-done.1
  31.7 5.7 %all-to-all-start = ((bf16[6,8,16,512]{3,1,0,2:T(8,128)(2,1)}), bf16[6,8,16,512]{3,1,0,2:T(8,128)(2,1)S(1)}, u32[]{:S(2)}, u32[]{:S(2)}) async-start(bf16[6,8,16,512]{3,1,0,2:T(8,128)(2,1)} %reshape.107), calls=%async_computation | async-start | bytes 1572864 | tf_op jit(solution)/shard_map/all_to_all | solution.py:80
  37.5 0.1 broadcast_and_fusion
  37.6 0.1 add.50
  37.7 18.9 %all-to-all-done = bf16[6,8,16,512]{3,1,0,2:T(8,128)(2,1)S(1)} async-done(((bf16[6,8,16,512]{3,1,0,2:T(8,128)(2,1)}), bf16[6,8,16,512]{3,1,0,2:T(8,128)(2,1)S(1)}, u32[]{:S(2)}, u32[]{:S(2)}) %all-to-all-start) | async-done | bytes 786464 | tf_op jit(solution)/shard_map/all_to_all | solution.py:80
  56.6 0.1 copy.41
  56.6 0.8 reshape.102
  57.5 1.1 %copy.51 = bf16[6,128,8,1,64]{1,2,4,0,3:T(8,128)(2,1)S(1)} copy(bf16[6,128,8,1,64]{4,2,1,0,3:T(8,128)(2,1)S(1)} %reshape.102) | data formatting | bytes 1572864
  58.6 0.1 pad.5.clone
  58.7 0.1 copy.44
  58.8 0.1 slice.28
  58.9 0.0 copy-start
  58.9 3.4 %all-gather.2.cloned.1.call-done = bf16[256,27,384]{2,0,1:T(8,128)(2,1)} async-done(((bf16[16,27,384]{2,0,1:T(8,128)(2,1)}), bf16[256,27,384]{2,0,1:T(8,128)(2,1)}) %all-gather.2.cloned.1.call-update) | async-done | bytes 5308432 | tf_op jit(solution)/shard_map/all_gather | solution.py:42
  62.3 0.0 slice-start
  62.3 0.0 copy-done
  62.3 1.5 %slice-done = bf16[256,27,128]{2,0,1:T(8,128)(2,1)S(1)} async-done(((bf16[256,27,384]{2,0,1:T(8,128)(2,1)}), bf16[256,27,128]{2,0,1:T(8,128)(2,1)S(1)}, s32[]{:S(2)}) %slice-start) | async-done | bytes 1769496 | tf_op jit(solution)/shard_map/slice | solution.py:45
  63.8 3.8 %fusion.6 = bf16[4,6,1,8,9,256]{5,3,4,1,0,2:T(8,128)(2,1)S(1)} fusion(bf16[256,3,3,3,128]{4,0,3,2,1:T(8,128)(2,1)S(1)} %bitcast.45, bf16[6,128,8,1,7,2]{1,4,5,2,0,3:T(8,128)(2,1)S(1)} %slice.28, bf16[6,128,8,1,8,9]{1,4,5,2,0,3:T(8,128)(2,1)S(1)} %copy.44, f32[256]{0:T(256)S(1)} %add.50, pred[8,9]{0,1:T(8,128)(4,1)S(1)} %copy-done, ...), kind=kOutput, calls=%fused_computation.12 | convolution fusion | flops 3064430592 | bytes 3712096 | tf_op jit(solution)/shard_map/conv_general_dilated | solution.py:18
  67.6 0.0 slice-start.1
  67.6 2.0 %slice-done.1 = bf16[256,27,256]{2,0,1:T(8,128)(2,1)S(1)} async-done(((bf16[256,27,384]{2,0,1:T(8,128)(2,1)}), bf16[256,27,256]{2,0,1:T(8,128)(2,1)S(1)}, s32[]{:S(2)}) %slice-start.1) | async-done | bytes 3538968 | tf_op jit(solution)/shard_map/slice | solution.py:46
  69.6 2.3 %fusion.9 = f32[2,4,8,9,256]{4,2,3,1,0:T(8,128)S(1)} fusion(bf16[256,3,3,3,256]{4,0,3,2,1:T(8,128)(2,1)S(1)} %bitcast.46, bf16[4,6,1,7,1,256]{5,3,4,1,0,2:T(8,128)(2,1)S(1)} %get-tuple-element.6, bf16[4,6,1,7,1,256]{5,3,4,1,0,2:T(8,128)(2,1)S(1)} %get-tuple-element.5, bf16[4,6,1,8,9,256]{5,3,4,1,0,2:T(8,128)(2,1)S(1)} %fusion.6), kind=kOutput, calls=%fused_computation.15 | convolution fusion | flops 2043838464 | bytes 5185536 | tf_op jit(solution)/shard_map/conv_general_dilated | solution.py:18
  71.9 0.2 copy.45
  72.2 0.4 copy.46
  72.6 0.6 squeeze.4
  73.2 0.1 fusion.26
  73.4 11.2 %all_to_all.35 = bf16[2,16,16,256]{3,2,0,1:T(8,128)(2,1)S(1)} all-to-all(bf16[2,16,16,256]{3,2,0,1:T(8,128)(2,1)S(1)} %copy.47), channel_id=1, replica_groups=mesh['depth'=16,'filt'=16] {'filt'}, dimensions={1} | all-to-all | bytes 524288 | tf_op jit(solution)/shard_map/all_to_all | solution.py:90
  84.6 0.1 copy.48
  84.7 0.8 reshape.91
  (6 shorter events, 0.1 us)
Async XLA Ops:
  6.5 55.8 %all-gather.2.cloned.1.call-start = ((), (), s32[]{:S(2)}) async-start(), calls=%async_computation.3 | async-start | bytes 5640192 | tf_op jit(solution)/shard_map/all_gather | solution.py:42
  8.3 17.4 %collective-permute-start = (bf16[2,8,4096]{2,1,0:T(8,128)(2,1)}, bf16[2,8,4096]{2,1,0:T(8,128)(2,1)S(1)}, u32[]{:S(2)}, u32[]{:S(2)}) collective-permute-start(bf16[2,8,4096]{2,1,0:T(8,128)(2,1)} %param.5), channel_id=1, source_target_pairs={{0,16},{16,32},{32,48},{48,64},{64,80},{80,96},{96,112},{112,128},... | collective-permute-start | bytes 393224 | tf_op jit(solution)/shard_map/ppermute | solution.py:33
  11.9 13.8 %collective-permute-start.1 = (bf16[2,8,4096]{2,1,0:T(8,128)(2,1)}, bf16[2,8,4096]{2,1,0:T(8,128)(2,1)S(1)}, u32[]{:S(2)}, u32[]{:S(2)}) collective-permute-start(bf16[2,8,4096]{2,1,0:T(8,128)(2,1)} %param.5), channel_id=1, source_target_pairs={{16,0},{32,16},{48,32},{64,48},{80,64},{96,80},{112,96},{128,112},... | collective-permute-start | bytes 393224 | tf_op jit(solution)/shard_map/ppermute | solution.py:34
  18.8 12.9 %all-to-all-start.1 = ((f32[16,2,16]{2,1,0:T(2,128)}), f32[16,2,16]{2,1,0:T(2,128)S(1)}, u32[]{:S(2)}, u32[]{:S(2)}) async-start(f32[16,2,16]{2,1,0:T(2,128)} %broadcast_in_dim.13), calls=%async_computation.1 | async-start | bytes 32768 | tf_op jit(solution)/shard_map/all_to_all | solution.py:54
  31.7 24.8 %all-to-all-start = ((bf16[6,8,16,512]{3,1,0,2:T(8,128)(2,1)}), bf16[6,8,16,512]{3,1,0,2:T(8,128)(2,1)S(1)}, u32[]{:S(2)}, u32[]{:S(2)}) async-start(bf16[6,8,16,512]{3,1,0,2:T(8,128)(2,1)} %reshape.107), calls=%async_computation | async-start | bytes 1572864 | tf_op jit(solution)/shard_map/all_to_all | solution.py:80
  58.9 3.4 %copy-start = (pred[8,9]{0,1:T(8,128)(4,1)S(1)}, pred[8,9]{0,1:T(8,128)(4,1)}, u32[]{:S(2)}) copy-start(pred[8,9]{0,1:T(8,128)(4,1)} %constant.42) | copy-start | bytes 220
  62.3 1.5 %slice-start = ((bf16[256,27,384]{2,0,1:T(8,128)(2,1)}), bf16[256,27,128]{2,0,1:T(8,128)(2,1)S(1)}, s32[]{:S(2)}) async-start(bf16[256,27,384]{2,0,1:T(8,128)(2,1)} %all-gather.2.cloned.1.call-done), calls=%async_computation.4 | async-start | bytes 3538944 | tf_op jit(solution)/shard_map/slice | solution.py:45
  67.6 2.0 %slice-start.1 = ((bf16[256,27,384]{2,0,1:T(8,128)(2,1)}), bf16[256,27,256]{2,0,1:T(8,128)(2,1)S(1)}, s32[]{:S(2)}) async-start(bf16[256,27,384]{2,0,1:T(8,128)(2,1)} %all-gather.2.cloned.1.call-done), calls=%async_computation.5 | async-start | bytes 7077888 | tf_op jit(solution)/shard_map/slice | solution.py:46
Sparse Core Ops, SparseCore 0:
  9.2 53.0 all-gather.1

commit v3 on v2

--- a/solution.py
+++ b/solution.py
@@ -20,7 +20,7 @@
         kernel,
         (1, 1, 1),
         ((0, 0), (0, 0), (1, 1)),
-        dimension_numbers=("NDCHW", "ODHWI", "NDCHW"),
+        dimension_numbers=("NDCHW", "DHWOI", "NDCHW"),
         preferred_element_type=jnp.float32,
     )
     return summed[0]
@@ -37,13 +37,14 @@
 
 def gather_kernels(first_kernel, second_kernel):
     outs, chans = first_kernel.shape[3], first_kernel.shape[4]
-    first = jnp.moveaxis(first_kernel.reshape(27, outs, chans), 1, 0)
-    second = jnp.moveaxis(second_kernel.reshape(27, outs, second_kernel.shape[4]), 1, 0)
-    whole = lax.all_gather(jnp.concatenate([first, second], axis=2), "filt", axis=0, tiled=True)
-    total = whole.shape[0]
+    joined = jnp.concatenate(
+        [first_kernel.reshape(27, outs, chans), second_kernel.reshape(27, outs, second_kernel.shape[4])], axis=2
+    )
+    whole = lax.all_gather(joined, "filt", axis=1, tiled=True)
+    total = whole.shape[1]
     return (
-        whole[:, :, :chans].reshape(total, 3, 3, 3, chans),
-        whole[:, :, chans:].reshape(total, 3, 3, 3, second_kernel.shape[4]),
+        whole[:, :, :chans].reshape(3, 3, 3, total, chans),
+        whole[:, :, chans:].reshape(3, 3, 3, total, second_kernel.shape[4]),
     )
 
 

time: 94.1 us -> 94.1 us (level)
  no operation moved by 1% of the time
where the time goes in v3:
time: 94.1 us; the launch traced here: 92.4 us
  waiting for transfers between devices  22.3 us (24%)
  starting transfers between devices  21.8 us (23%)
  between operations  13.6 us (14%)
  local copies, waits for them, and re-layouts  13.4 us (14%)
  blocking collectives  11.2 us (12%)
  matrix products  6.06 us (6%)
  other arithmetic  3.95 us (4%)
    all_to_all x1, waiting for transfers between devices, local(): mine = lax.all_to_all(windows, 'filt', 2, 1, tiled=True)  18.9 us
    all_to_all x1, blocking collectives, local(): result = lax.all_to_all(second, 'filt', 1, 3, tiled=True)  11.2 us
    all_to_all x1, starting transfers between devices, gather_biases(): whole = lax.all_to_all(spread, 'filt', 0, 0, tiled=True)  6.88 us
    conv_general_dilated x2, matrix products, conv(): lax.conv_general_dilated(framed[None], kernel, (1, 1, 1), ((0, 0), (0, 0)...  6.06 us
    all_to_all x1, starting transfers between devices, local(): mine = lax.all_to_all(windows, 'filt', 2, 1, tiled=True)  5.72 us
    ppermute x1, starting transfers between devices, depth_halo(): high = lax.ppermute(block[:reach], 'depth', backward)  5.63 us
    ppermute x1, starting transfers between devices, depth_halo(): low = lax.ppermute(block[block.shape[0] - reach:], 'depth', forward)  3.55 us
    all_gather x1, waiting for transfers between devices, gather_kernels(): whole = lax.all_gather(joined, 'filt', axis=1, tiled=True)  3.42 us
  transfers between devices with their start and end apart: 5, of which 2 were waited for; matrix products, arithmetic and copies ran while one was open for 10% of the time, Pallas kernels for 0%

profile of v3, /device:TPU:17, one launch (start us, length us, event | category | flops | bytes accessed | tf_op | source)
XLA Modules:
  0.0 92.4 jit_solution(1947402109707797569)
XLA Ops:
  6.5 0.0 all-gather.2.cloned.1.call-start
  6.5 1.8 %pad_maximum_fusion.2 = bf16[27,16,384]{2,1,0:T(8,128)(2,1)} fusion(bf16[27,16,256]{2,1,0:T(8,128)(2,1)} %bitcast.49, bf16[27,16,128]{2,1,0:T(8,128)(2,1)} %bitcast.50), kind=kLoop, calls=%fused_computation.34 | loop fusion | flops 663552 | bytes 663552 | tf_op jit(solution)/shard_map/concatenate | solution.py:40
  8.3 0.0 all-gather.2.cloned.1.call-update
  8.3 3.5 %collective-permute-start = (bf16[2,8,4096]{2,1,0:T(8,128)(2,1)}, bf16[2,8,4096]{2,1,0:T(8,128)(2,1)S(1)}, u32[]{:S(2)}, u32[]{:S(2)}) collective-permute-start(bf16[2,8,4096]{2,1,0:T(8,128)(2,1)} %param.5), channel_id=1, source_target_pairs={{0,16},{16,32},{32,48},{48,64},{64,80},{80,96},{96,112},{112,128},... | collective-permute-start | bytes 393224 | tf_op jit(solution)/shard_map/ppermute | solution.py:33
  11.9 5.6 %collective-permute-start.1 = (bf16[2,8,4096]{2,1,0:T(8,128)(2,1)}, bf16[2,8,4096]{2,1,0:T(8,128)(2,1)S(1)}, u32[]{:S(2)}, u32[]{:S(2)}) collective-permute-start(bf16[2,8,4096]{2,1,0:T(8,128)(2,1)} %param.5), channel_id=1, source_target_pairs={{16,0},{32,16},{48,32},{64,48},{80,64},{96,80},{112,96},{128,112},... | collective-permute-start | bytes 393224 | tf_op jit(solution)/shard_map/ppermute | solution.py:34
  17.5 0.7 pad_maximum_fusion.3
  18.2 0.6 broadcast_in_dim.13
  18.8 6.9 %all-to-all-start.1 = ((f32[16,2,16]{2,1,0:T(2,128)}), f32[16,2,16]{2,1,0:T(2,128)S(1)}, u32[]{:S(2)}, u32[]{:S(2)}) async-start(f32[16,2,16]{2,1,0:T(2,128)} %broadcast_in_dim.13), calls=%async_computation.1 | async-start | bytes 32768 | tf_op jit(solution)/shard_map/all_to_all | solution.py:55
  25.7 0.0 collective-permute-done
  25.7 0.0 collective-permute-done.1
  25.7 1.0 %pad_maximum_fusion.1 = bf16[6,8,4096]{2,1,0:T(8,128)(2,1)S(1)} fusion(bf16[2,8,4096]{2,1,0:T(8,128)(2,1)S(1)} %collective-permute-done.1, bf16[2,8,4096]{2,1,0:T(8,128)(2,1)} %param.5, bf16[2,8,4096]{2,1,0:T(8,128)(2,1)S(1)} %collective-permute-done), kind=kLoop, calls=%fused_computation.33 | loop fusion | flops 393216 | bytes 786432 | tf_op jit(solution)/shard_map/concatenate | solution.py:35
  26.7 0.8 reshape.83
  27.5 0.7 pad_slice_fusion.1
  28.2 0.5 copy.37
  28.7 0.5 copy.38
  29.3 0.3 pad_maximum_fusion
  29.6 0.5 copy.49
  30.0 1.7 %reshape.107 = bf16[6,8,16,512]{3,1,0,2:T(8,128)(2,1)} reshape(bf16[6,8,16,8,64]{4,3,1,0,2:T(8,128)(2,1)S(1)} %copy.49) | data formatting | bytes 1572864 | tf_op jit(solution)/shard_map/reshape | solution.py:80
  31.7 0.0 all-to-all-done.1
  31.7 5.7 %all-to-all-start = ((bf16[6,8,16,512]{3,1,0,2:T(8,128)(2,1)}), bf16[6,8,16,512]{3,1,0,2:T(8,128)(2,1)S(1)}, u32[]{:S(2)}, u32[]{:S(2)}) async-start(bf16[6,8,16,512]{3,1,0,2:T(8,128)(2,1)} %reshape.107), calls=%async_computation | async-start | bytes 1572864 | tf_op jit(solution)/shard_map/all_to_all | solution.py:81
  37.5 0.1 broadcast_and_fusion
  37.6 0.1 add.50
  37.7 18.9 %all-to-all-done = bf16[6,8,16,512]{3,1,0,2:T(8,128)(2,1)S(1)} async-done(((bf16[6,8,16,512]{3,1,0,2:T(8,128)(2,1)}), bf16[6,8,16,512]{3,1,0,2:T(8,128)(2,1)S(1)}, u32[]{:S(2)}, u32[]{:S(2)}) %all-to-all-start) | async-done | bytes 786464 | tf_op jit(solution)/shard_map/all_to_all | solution.py:81
  56.6 0.1 copy.41
  56.6 0.8 reshape.102
  57.5 1.1 %copy.51 = bf16[6,128,8,1,64]{1,2,4,0,3:T(8,128)(2,1)S(1)} copy(bf16[6,128,8,1,64]{4,2,1,0,3:T(8,128)(2,1)S(1)} %reshape.102) | data formatting | bytes 1572864
  58.6 0.1 pad.5.clone
  58.7 0.1 copy.44
  58.8 0.1 slice.28
  58.9 0.0 copy-start
  58.9 3.4 %all-gather.2.cloned.1.call-done = bf16[27,256,384]{2,1,0:T(8,128)(2,1)} async-done(((bf16[27,16,384]{2,1,0:T(8,128)(2,1)}), bf16[27,256,384]{2,1,0:T(8,128)(2,1)}) %all-gather.2.cloned.1.call-update) | async-done | bytes 5308432 | tf_op jit(solution)/shard_map/all_gather | solution.py:43
  62.3 0.0 slice-start
  62.3 0.0 copy-done
  62.3 1.5 %slice-done = bf16[27,256,128]{2,1,0:T(8,128)(2,1)S(1)} async-done(((bf16[27,256,384]{2,1,0:T(8,128)(2,1)}), bf16[27,256,128]{2,1,0:T(8,128)(2,1)S(1)}, s32[]{:S(2)}) %slice-start) | async-done | bytes 1769496 | tf_op jit(solution)/shard_map/slice | solution.py:46
  63.8 3.8 %fusion.6 = bf16[4,6,1,8,9,256]{5,3,4,1,0,2:T(8,128)(2,1)S(1)} fusion(bf16[3,3,3,256,128]{4,3,2,1,0:T(8,128)(2,1)S(1)} %bitcast.41, bf16[6,128,8,1,7,2]{1,4,5,2,0,3:T(8,128)(2,1)S(1)} %slice.28, bf16[6,128,8,1,8,9]{1,4,5,2,0,3:T(8,128)(2,1)S(1)} %copy.44, f32[256]{0:T(256)S(1)} %add.50, pred[8,9]{0,1:T(8,128)(4,1)S(1)} %copy-done, ...), kind=kOutput, calls=%fused_computation.12 | convolution fusion | flops 3064430592 | bytes 3712096 | tf_op jit(solution)/shard_map/conv_general_dilated | solution.py:18
  67.6 0.0 slice-start.1
  67.6 2.0 %slice-done.1 = bf16[27,256,256]{2,1,0:T(8,128)(2,1)S(1)} async-done(((bf16[27,256,384]{2,1,0:T(8,128)(2,1)}), bf16[27,256,256]{2,1,0:T(8,128)(2,1)S(1)}, s32[]{:S(2)}) %slice-start.1) | async-done | bytes 3538968 | tf_op jit(solution)/shard_map/slice | solution.py:47
  69.6 2.3 %fusion.9 = f32[2,4,8,9,256]{4,2,3,1,0:T(8,128)S(1)} fusion(bf16[3,3,3,256,256]{4,3,2,1,0:T(8,128)(2,1)S(1)} %bitcast.42, bf16[4,6,1,7,1,256]{5,3,4,1,0,2:T(8,128)(2,1)S(1)} %get-tuple-element.6, bf16[4,6,1,7,1,256]{5,3,4,1,0,2:T(8,128)(2,1)S(1)} %get-tuple-element.5, bf16[4,6,1,8,9,256]{5,3,4,1,0,2:T(8,128)(2,1)S(1)} %fusion.6), kind=kOutput, calls=%fused_computation.15 | convolution fusion | flops 2043838464 | bytes 5185536 | tf_op jit(solution)/shard_map/conv_general_dilated | solution.py:18
  71.9 0.2 copy.45
  72.2 0.4 copy.46
  72.6 0.6 squeeze.4
  73.2 0.1 fusion.26
  73.4 11.2 %all_to_all.35 = bf16[2,16,16,256]{3,2,0,1:T(8,128)(2,1)S(1)} all-to-all(bf16[2,16,16,256]{3,2,0,1:T(8,128)(2,1)S(1)} %copy.47), channel_id=1, replica_groups=mesh['depth'=16,'filt'=16] {'filt'}, dimensions={1} | all-to-all | bytes 524288 | tf_op jit(solution)/shard_map/all_to_all | solution.py:91
  84.6 0.1 copy.48
  84.7 0.8 reshape.91
  (6 shorter events, 0.1 us)
Async XLA Ops:
  6.5 55.8 %all-gather.2.cloned.1.call-start = ((), (), s32[]{:S(2)}) async-start(), calls=%async_computation.3 | async-start | bytes 5640192 | tf_op jit(solution)/shard_map/all_gather | solution.py:43
  8.3 17.4 %collective-permute-start = (bf16[2,8,4096]{2,1,0:T(8,128)(2,1)}, bf16[2,8,4096]{2,1,0:T(8,128)(2,1)S(1)}, u32[]{:S(2)}, u32[]{:S(2)}) collective-permute-start(bf16[2,8,4096]{2,1,0:T(8,128)(2,1)} %param.5), channel_id=1, source_target_pairs={{0,16},{16,32},{32,48},{48,64},{64,80},{80,96},{96,112},{112,128},... | collective-permute-start | bytes 393224 | tf_op jit(solution)/shard_map/ppermute | solution.py:33
  11.9 13.8 %collective-permute-start.1 = (bf16[2,8,4096]{2,1,0:T(8,128)(2,1)}, bf16[2,8,4096]{2,1,0:T(8,128)(2,1)S(1)}, u32[]{:S(2)}, u32[]{:S(2)}) collective-permute-start(bf16[2,8,4096]{2,1,0:T(8,128)(2,1)} %param.5), channel_id=1, source_target_pairs={{16,0},{32,16},{48,32},{64,48},{80,64},{96,80},{112,96},{128,112},... | collective-permute-start | bytes 393224 | tf_op jit(solution)/shard_map/ppermute | solution.py:34
  18.8 12.9 %all-to-all-start.1 = ((f32[16,2,16]{2,1,0:T(2,128)}), f32[16,2,16]{2,1,0:T(2,128)S(1)}, u32[]{:S(2)}, u32[]{:S(2)}) async-start(f32[16,2,16]{2,1,0:T(2,128)} %broadcast_in_dim.13), calls=%async_computation.1 | async-start | bytes 32768 | tf_op jit(solution)/shard_map/all_to_all | solution.py:55
  31.7 24.8 %all-to-all-start = ((bf16[6,8,16,512]{3,1,0,2:T(8,128)(2,1)}), bf16[6,8,16,512]{3,1,0,2:T(8,128)(2,1)S(1)}, u32[]{:S(2)}, u32[]{:S(2)}) async-start(bf16[6,8,16,512]{3,1,0,2:T(8,128)(2,1)} %reshape.107), calls=%async_computation | async-start | bytes 1572864 | tf_op jit(solution)/shard_map/all_to_all | solution.py:81
  58.9 3.4 %copy-start = (pred[8,9]{0,1:T(8,128)(4,1)S(1)}, pred[8,9]{0,1:T(8,128)(4,1)}, u32[]{:S(2)}) copy-start(pred[8,9]{0,1:T(8,128)(4,1)} %constant.42) | copy-start | bytes 220
  62.3 1.5 %slice-start = ((bf16[27,256,384]{2,1,0:T(8,128)(2,1)}), bf16[27,256,128]{2,1,0:T(8,128)(2,1)S(1)}, s32[]{:S(2)}) async-start(bf16[27,256,384]{2,1,0:T(8,128)(2,1)} %all-gather.2.cloned.1.call-done), calls=%async_computation.4 | async-start | bytes 3538944 | tf_op jit(solution)/shard_map/slice | solution.py:46
  67.6 2.0 %slice-start.1 = ((bf16[27,256,384]{2,1,0:T(8,128)(2,1)}), bf16[27,256,256]{2,1,0:T(8,128)(2,1)S(1)}, s32[]{:S(2)}) async-start(bf16[27,256,384]{2,1,0:T(8,128)(2,1)} %all-gather.2.cloned.1.call-done), calls=%async_computation.5 | async-start | bytes 7077888 | tf_op jit(solution)/shard_map/slice | solution.py:47
Sparse Core Ops, SparseCore 0:
  9.2 53.0 all-gather.1

commit v4 on v2

--- a/solution.py
+++ b/solution.py
@@ -71,14 +71,13 @@
     kernel_1, kernel_2 = gather_kernels(first_kernel, second_kernel)
     bias_1, bias_2 = gather_biases(first_bias, second_bias)
 
-    extended = depth_halo(features, 2).reshape(planes + 4, chans, rows, SIDE)
-    framed = jnp.pad(extended, ((0, 0), (0, 0), (2, max(2, block_rows)), (0, 0)))
-    heads = framed[:, :, :rows].reshape(planes + 4, chans, count, block_rows, SIDE)
-    tails = framed[:, :, block_rows : rows + block_rows].reshape(planes + 4, chans, count, block_rows, SIDE)
-    windows = jnp.concatenate([heads, tails[:, :, :, : 4]], axis=3)
-    windows = windows.reshape(planes + 4, chans, count, (block_rows + 4) * SIDE)
+    framed = jnp.pad(features.reshape(planes, chans, rows, SIDE), ((0, 0), (0, 0), (2, max(2, block_rows)), (0, 0)))
+    heads = framed[:, :, :rows].reshape(planes, chans, count, block_rows, SIDE)
+    tails = framed[:, :, block_rows : rows + block_rows].reshape(planes, chans, count, block_rows, SIDE)
+    windows = jnp.concatenate([heads, tails[:, :, :, :4]], axis=3)
+    windows = windows.reshape(planes, chans, count, (block_rows + 4) * SIDE)
     mine = lax.all_to_all(windows, "filt", 2, 1, tiled=True)
-    mine = mine.reshape(planes + 4, count * chans, block_rows + 4, SIDE)
+    mine = depth_halo(mine.reshape(planes, count * chans, block_rows + 4, SIDE), 2)
 
     hidden = activate(conv(mine, kernel_1), bias_1)
     grid = inside(planes * lax.axis_size("depth"), rows, planes, block_rows)

time: 94.1 us -> 96.9 us (1.030)
  the two profiles are of different devices: /device:TPU:17 before, /device:TPU:1 now
where the time goes in v4:
time: 96.9 us; the launch traced here: 96.5 us
  waiting for transfers between devices  37 us (38%)
  starting transfers between devices  15.4 us (16%)
  between operations  13.6 us (14%)
  local copies, waits for them, and re-layouts  11 us (11%)
  blocking collectives  11 us (11%)
  matrix products  6.05 us (6%)
  other arithmetic  2.48 us (3%)
    all_gather x1, waiting for transfers between devices, gather_kernels(): lax.all_gather(jnp.concatenate([first, second], axis=2), 'filt', axis=0,...  15.8 us
    all_to_all x1, blocking collectives, local(): result = lax.all_to_all(second, 'filt', 1, 3, tiled=True)  11 us
    ppermute x1, waiting for transfers between devices, depth_halo(): low = lax.ppermute(block[block.shape[0] - reach:], 'depth', forward)  8.97 us
    all_to_all x1, waiting for transfers between devices, local(): mine = lax.all_to_all(windows, 'filt', 2, 1, tiled=True)  7.34 us
    all_to_all x1, starting transfers between devices, local(): mine = lax.all_to_all(windows, 'filt', 2, 1, tiled=True)  6.83 us
    conv_general_dilated x2, matrix products, conv(): lax.conv_general_dilated(framed[None], kernel, (1, 1, 1), ((0, 0), (0, 0)...  6.05 us
    ppermute x1, waiting for transfers between devices, depth_halo(): high = lax.ppermute(block[:reach], 'depth', backward)  4.25 us
    all_to_all x1, starting transfers between devices, gather_biases(): whole = lax.all_to_all(spread, 'filt', 0, 0, tiled=True)  3.68 us
  transfers between devices with their start and end apart: 5, of which 5 were waited for; matrix products, arithmetic and copies ran while one was open for 6% of the time, Pallas kernels for 0%

profile of v4, /device:TPU:1, one launch (start us, length us, event | category | flops | bytes accessed | tf_op | source)
XLA Modules:
  0.0 96.5 jit_solution(11746301106283718439)
XLA Ops:
  6.5 0.0 all-gather.2.cloned.1.call-start
  6.5 1.8 %pad_maximum_fusion.1 = bf16[16,27,384]{2,0,1:T(8,128)(2,1)} fusion(bf16[16,27,256]{2,0,1:T(8,128)(2,1)} %bitcast.55, bf16[16,27,128]{2,0,1:T(8,128)(2,1)} %bitcast.56), kind=kLoop, calls=%fused_computation.32 | loop fusion | flops 663552 | bytes 663552 | tf_op jit(solution)/shard_map/concatenate | solution.py:42
  8.3 0.0 all-gather.2.cloned.1.call-update
  8.4 1.2 %reshape.86 = bf16[2,8,64,64]{3,2,1,0:T(8,128)(2,1)S(1)} reshape(bf16[2,8,4096]{2,1,0:T(8,128)(2,1)} %param.5) | data formatting | bytes 262144 | tf_op jit(solution)/shard_map/reshape | solution.py:74
  9.5 0.2 pad_slice_fusion.1
  9.7 0.2 copy.37
  9.9 0.2 copy.38
  10.1 0.0 copy-start
  10.1 0.0 copy-start.1
  10.1 0.1 pad_maximum_fusion
  10.2 0.1 copy.49
  10.3 1.0 %reshape.111 = bf16[2,8,16,512]{3,1,0,2:T(8,128)(2,1)} reshape(bf16[2,8,16,8,64]{4,3,1,0,2:T(8,128)(2,1)S(1)} %copy.49) | data formatting | bytes 524288 | tf_op jit(solution)/shard_map/reshape | solution.py:78
  11.3 6.8 %all-to-all-start = ((bf16[2,8,16,512]{3,1,0,2:T(8,128)(2,1)}), bf16[2,8,16,512]{3,1,0,2:T(8,128)(2,1)S(1)}, u32[]{:S(2)}, u32[]{:S(2)}) async-start(bf16[2,8,16,512]{3,1,0,2:T(8,128)(2,1)} %reshape.111), calls=%async_computation | async-start | bytes 524288 | tf_op jit(solution)/shard_map/all_to_all | solution.py:79
  18.2 0.0 copy-done
  18.2 0.0 copy-done.1
  18.2 7.3 %all-to-all-done = bf16[2,8,16,512]{3,1,0,2:T(8,128)(2,1)S(1)} async-done(((bf16[2,8,16,512]{3,1,0,2:T(8,128)(2,1)}), bf16[2,8,16,512]{3,1,0,2:T(8,128)(2,1)S(1)}, u32[]{:S(2)}, u32[]{:S(2)}) %all-to-all-start) | async-done | bytes 262176 | tf_op jit(solution)/shard_map/all_to_all | solution.py:79
  25.6 0.6 broadcast_in_dim.25
  26.2 3.7 %all-to-all-start.1 = ((f32[16,2,16]{2,1,0:T(2,128)}), f32[16,2,16]{2,1,0:T(2,128)S(1)}, u32[]{:S(2)}, u32[]{:S(2)}) async-start(f32[16,2,16]{2,1,0:T(2,128)} %broadcast_in_dim.25), calls=%async_computation.1 | async-start | bytes 32768 | tf_op jit(solution)/shard_map/all_to_all | solution.py:54
  29.9 0.3 reshape.90
  30.2 3.6 %collective-permute-start = (bf16[2,128,8,64]{3,2,1,0:T(8,128)(2,1)S(1)}, bf16[2,128,8,64]{3,2,1,0:T(8,128)(2,1)S(1)}, u32[]{:S(2)}, u32[]{:S(2)}) collective-permute-start(bf16[2,128,8,64]{3,2,1,0:T(8,128)(2,1)S(1)} %reshape.90), channel_id=1, source_target_pairs={{0,16},{16,32},{32,48},{48,64},{64,80},{80,96},{96,112},{112,128},... | collective-permute-start | bytes 786440 | tf_op jit(solution)/shard_map/ppermute | solution.py:33
  33.8 1.3 %collective-permute-start.1 = (bf16[2,128,8,64]{3,2,1,0:T(8,128)(2,1)S(1)}, bf16[2,128,8,64]{3,2,1,0:T(8,128)(2,1)S(1)}, u32[]{:S(2)}, u32[]{:S(2)}) collective-permute-start(bf16[2,128,8,64]{3,2,1,0:T(8,128)(2,1)S(1)} %reshape.90), channel_id=1, source_target_pairs={{16,0},{32,16},{48,32},{64,48},{80,64},{96,80},{112,96},{128,112},... | collective-permute-start | bytes 786440 | tf_op jit(solution)/shard_map/ppermute | solution.py:34
  35.1 0.1 broadcast_and_fusion
  35.1 0.6 all-to-all-done.1
  35.8 0.1 add.50
  35.8 9.0 %collective-permute-done = bf16[2,128,8,64]{3,2,1,0:T(8,128)(2,1)S(1)} collective-permute-done((bf16[2,128,8,64]{3,2,1,0:T(8,128)(2,1)S(1)}, bf16[2,128,8,64]{3,2,1,0:T(8,128)(2,1)S(1)}, u32[]{:S(2)}, u32[]{:S(2)}) %collective-permute-start) | collective-permute-done | bytes 262176 | tf_op jit(solution)/shard_map/ppermute | solution.py:33
  44.8 4.2 %collective-permute-done.1 = bf16[2,128,8,64]{3,2,1,0:T(8,128)(2,1)S(1)} collective-permute-done((bf16[2,128,8,64]{3,2,1,0:T(8,128)(2,1)S(1)}, bf16[2,128,8,64]{3,2,1,0:T(8,128)(2,1)S(1)}, u32[]{:S(2)}, u32[]{:S(2)}) %collective-permute-start.1) | collective-permute-done | bytes 262176 | tf_op jit(solution)/shard_map/ppermute | solution.py:34
  49.1 0.3 maximum_bitcast_fusion
  49.4 1.1 %copy.51 = bf16[6,128,8,1,64]{1,2,4,0,3:T(8,128)(2,1)S(1)} copy(bf16[6,128,8,1,64]{4,2,1,0,3:T(8,128)(2,1)S(1)} %maximum_bitcast_fusion) | data formatting | bytes 1572864
  50.5 0.1 pad.5.clone
  50.6 0.1 copy.44
  50.7 0.1 slice.28
  50.8 0.0 copy-start.2
  50.8 15.8 %all-gather.2.cloned.1.call-done = bf16[256,27,384]{2,0,1:T(8,128)(2,1)} async-done(((bf16[16,27,384]{2,0,1:T(8,128)(2,1)}), bf16[256,27,384]{2,0,1:T(8,128)(2,1)}) %all-gather.2.cloned.1.call-update) | async-done | bytes 5308432 | tf_op jit(solution)/shard_map/all_gather | solution.py:42
  66.6 0.0 slice-start
  66.6 0.0 copy-done.2
  66.6 1.5 %slice-done = bf16[256,27,128]{2,0,1:T(8,128)(2,1)S(1)} async-done(((bf16[256,27,384]{2,0,1:T(8,128)(2,1)}), bf16[256,27,128]{2,0,1:T(8,128)(2,1)S(1)}, s32[]{:S(2)}) %slice-start) | async-done | bytes 1769496 | tf_op jit(solution)/shard_map/slice | solution.py:45
  68.1 3.8 %fusion.6 = bf16[4,6,1,8,9,256]{5,3,4,1,0,2:T(8,128)(2,1)S(1)} fusion(bf16[256,3,3,3,128]{4,0,3,2,1:T(8,128)(2,1)S(1)} %bitcast.47, bf16[6,128,8,1,7,2]{1,4,5,2,0,3:T(8,128)(2,1)S(1)} %slice.28, bf16[6,128,8,1,8,9]{1,4,5,2,0,3:T(8,128)(2,1)S(1)} %copy.44, f32[256]{0:T(256)S(1)} %add.50, pred[8,9]{0,1:T(8,128)(4,1)S(1)} %copy-done.2, ...), kind=kOutput, calls=%fused_computation.12 | convolution fusion | flops 3064430592 | bytes 3712096 | tf_op jit(solution)/shard_map/conv_general_dilated | solution.py:18
  71.9 0.0 slice-start.1
  71.9 2.0 %slice-done.1 = bf16[256,27,256]{2,0,1:T(8,128)(2,1)S(1)} async-done(((bf16[256,27,384]{2,0,1:T(8,128)(2,1)}), bf16[256,27,256]{2,0,1:T(8,128)(2,1)S(1)}, s32[]{:S(2)}) %slice-start.1) | async-done | bytes 3538968 | tf_op jit(solution)/shard_map/slice | solution.py:46
  73.9 2.3 %fusion.9 = f32[2,4,8,9,256]{4,2,3,1,0:T(8,128)S(1)} fusion(bf16[256,3,3,3,256]{4,0,3,2,1:T(8,128)(2,1)S(1)} %bitcast.48, bf16[4,6,1,7,1,256]{5,3,4,1,0,2:T(8,128)(2,1)S(1)} %get-tuple-element.6, bf16[4,6,1,7,1,256]{5,3,4,1,0,2:T(8,128)(2,1)S(1)} %get-tuple-element.5, bf16[4,6,1,8,9,256]{5,3,4,1,0,2:T(8,128)(2,1)S(1)} %fusion.6), kind=kOutput, calls=%fused_computation.15 | convolution fusion | flops 2043838464 | bytes 5185536 | tf_op jit(solution)/shard_map/conv_general_dilated | solution.py:18
  76.2 0.2 copy.45
  76.5 0.4 copy.46
  76.9 0.6 squeeze.4
  77.5 0.1 fusion.26
  77.7 11.0 %all_to_all.35 = bf16[2,16,16,256]{3,2,0,1:T(8,128)(2,1)S(1)} all-to-all(bf16[2,16,16,256]{3,2,0,1:T(8,128)(2,1)S(1)} %copy.47), channel_id=1, replica_groups=mesh['depth'=16,'filt'=16] {'filt'}, dimensions={1} | all-to-all | bytes 524288 | tf_op jit(solution)/shard_map/all_to_all | solution.py:89
  88.6 0.1 copy.48
  88.8 0.8 reshape.95
  (8 shorter events, 0.2 us)
Async XLA Ops:
  6.5 60.1 %all-gather.2.cloned.1.call-start = ((), (), s32[]{:S(2)}) async-start(), calls=%async_computation.3 | async-start | bytes 5640192 | tf_op jit(solution)/shard_map/all_gather | solution.py:42
  10.1 8.1 %copy-start = (f32[16]{0:T(128)S(1)}, f32[16]{0:T(128)}, u32[]{:S(2)}) copy-start(f32[16]{0:T(128)} %param.9) | copy-start | bytes 196
  10.1 8.1 %copy-start.1 = (f32[16]{0:T(128)S(1)}, f32[16]{0:T(128)}, u32[]{:S(2)}) copy-start(f32[16]{0:T(128)} %param.7) | copy-start | bytes 196
  11.3 14.2 %all-to-all-start = ((bf16[2,8,16,512]{3,1,0,2:T(8,128)(2,1)}), bf16[2,8,16,512]{3,1,0,2:T(8,128)(2,1)S(1)}, u32[]{:S(2)}, u32[]{:S(2)}) async-start(bf16[2,8,16,512]{3,1,0,2:T(8,128)(2,1)} %reshape.111), calls=%async_computation | async-start | bytes 524288 | tf_op jit(solution)/shard_map/all_to_all | solution.py:79
  26.2 9.5 %all-to-all-start.1 = ((f32[16,2,16]{2,1,0:T(2,128)}), f32[16,2,16]{2,1,0:T(2,128)S(1)}, u32[]{:S(2)}, u32[]{:S(2)}) async-start(f32[16,2,16]{2,1,0:T(2,128)} %broadcast_in_dim.25), calls=%async_computation.1 | async-start | bytes 32768 | tf_op jit(solution)/shard_map/all_to_all | solution.py:54
  30.2 14.6 %collective-permute-start = (bf16[2,128,8,64]{3,2,1,0:T(8,128)(2,1)S(1)}, bf16[2,128,8,64]{3,2,1,0:T(8,128)(2,1)S(1)}, u32[]{:S(2)}, u32[]{:S(2)}) collective-permute-start(bf16[2,128,8,64]{3,2,1,0:T(8,128)(2,1)S(1)} %reshape.90), channel_id=1, source_target_pairs={{0,16},{16,32},{32,48},{48,64},{64,80},{80,96},{96,112},{112,128},... | collective-permute-start | bytes 786440 | tf_op jit(solution)/shard_map/ppermute | solution.py:33
  33.8 15.3 %collective-permute-start.1 = (bf16[2,128,8,64]{3,2,1,0:T(8,128)(2,1)S(1)}, bf16[2,128,8,64]{3,2,1,0:T(8,128)(2,1)S(1)}, u32[]{:S(2)}, u32[]{:S(2)}) collective-permute-start(bf16[2,128,8,64]{3,2,1,0:T(8,128)(2,1)S(1)} %reshape.90), channel_id=1, source_target_pairs={{16,0},{32,16},{48,32},{64,48},{80,64},{96,80},{112,96},{128,112},... | collective-permute-start | bytes 786440 | tf_op jit(solution)/shard_map/ppermute | solution.py:34
  50.8 15.8 %copy-start.2 = (pred[8,9]{0,1:T(8,128)(4,1)S(1)}, pred[8,9]{0,1:T(8,128)(4,1)}, u32[]{:S(2)}) copy-start(pred[8,9]{0,1:T(8,128)(4,1)} %constant.42) | copy-start | bytes 220
  66.6 1.5 %slice-start = ((bf16[256,27,384]{2,0,1:T(8,128)(2,1)}), bf16[256,27,128]{2,0,1:T(8,128)(2,1)S(1)}, s32[]{:S(2)}) async-start(bf16[256,27,384]{2,0,1:T(8,128)(2,1)} %all-gather.2.cloned.1.call-done), calls=%async_computation.4 | async-start | bytes 3538944 | tf_op jit(solution)/shard_map/slice | solution.py:45
  71.9 2.0 %slice-start.1 = ((bf16[256,27,384]{2,0,1:T(8,128)(2,1)}), bf16[256,27,256]{2,0,1:T(8,128)(2,1)S(1)}, s32[]{:S(2)}) async-start(bf16[256,27,384]{2,0,1:T(8,128)(2,1)} %all-gather.2.cloned.1.call-done), calls=%async_computation.5 | async-start | bytes 7077888 | tf_op jit(solution)/shard_map/slice | solution.py:46
Sparse Core Ops, SparseCore 0:
  9.2 57.3 all-gather.1

commit v5 on v2

--- a/solution.py
+++ b/solution.py
@@ -83,7 +83,9 @@
     hidden = activate(conv(mine, kernel_1), bias_1)
     grid = inside(planes * lax.axis_size("depth"), rows, planes, block_rows)
     hidden = jnp.where(grid, hidden, jnp.zeros_like(hidden))
-    second = activate(conv(hidden, kernel_2), bias_2)
+    half = kernel_2.shape[0] // 2
+    second = jnp.concatenate([conv(hidden, kernel_2[:half]), conv(hidden, kernel_2[half:])], axis=1)
+    second = activate(second, bias_2)
 
     outs = second_kernel.shape[3]
     second = second.reshape(planes, count, outs, block_rows * SIDE)

time: 94.1 us -> 94.5 us (level)
  matrix products: 6.06 us -> 8.17 us
  local copies, waits for them, and re-layouts: 13.4 us -> 11.7 us
    conv_general_dilated x2 -> x3, matrix products: 6.06 us -> 8.17 us  [conv(): lax.conv_general_dilated(framed[None], kernel, (1, 1, 1), ((0, 0), (0, 0)...]
    slice x2 -> x1, local copies, waits for them, and re-layouts: 1.99 us -> 0.31 us  [local(): kernel_2[:half]]
    concatenate x0 -> x2, local copies, waits for them, and re-layouts: none -> 1.01 us  [local(): jnp.concatenate([conv(hidden, kernel_2[:half]), conv(hidden, kernel_2[hal...]
where the time goes in v5:
time: 94.5 us; the launch traced here: 92.9 us
  waiting for transfers between devices  22.3 us (24%)
  starting transfers between devices  21.8 us (23%)
  between operations  13.7 us (14%)
  local copies, waits for them, and re-layouts  11.7 us (12%)
  blocking collectives  11.2 us (12%)
  matrix products  8.17 us (9%)
  other arithmetic  4.06 us (4%)
    all_to_all x1, waiting for transfers between devices, local(): mine = lax.all_to_all(windows, 'filt', 2, 1, tiled=True)  18.9 us
    all_to_all x1, blocking collectives, local(): result = lax.all_to_all(second, 'filt', 1, 3, tiled=True)  11.2 us
    conv_general_dilated x3, matrix products, conv(): lax.conv_general_dilated(framed[None], kernel, (1, 1, 1), ((0, 0), (0, 0)...  8.17 us
    all_to_all x1, starting transfers between devices, gather_biases(): whole = lax.all_to_all(spread, 'filt', 0, 0, tiled=True)  6.88 us
    all_to_all x1, starting transfers between devices, local(): mine = lax.all_to_all(windows, 'filt', 2, 1, tiled=True)  5.72 us
    ppermute x1, starting transfers between devices, depth_halo(): high = lax.ppermute(block[:reach], 'depth', backward)  5.63 us
    ppermute x1, starting transfers between devices, depth_halo(): low = lax.ppermute(block[block.shape[0] - reach:], 'depth', forward)  3.55 us
    all_gather x1, waiting for transfers between devices, gather_kernels(): lax.all_gather(jnp.concatenate([first, second], axis=2), 'filt', axis=0,...  3.42 us
  transfers between devices with their start and end apart: 5, of which 2 were waited for; matrix products, arithmetic and copies ran while one was open for 10% of the time, Pallas kernels for 0%

profile of v5, /device:TPU:17, one launch (start us, length us, event | category | flops | bytes accessed | tf_op | source)
XLA Modules:
  0.0 92.9 jit_solution(2166474288253203248)
XLA Ops:
  6.5 0.0 all-gather.2.cloned.1.call-start
  6.5 1.8 %pad_maximum_fusion.3 = bf16[16,27,384]{2,0,1:T(8,128)(2,1)} fusion(bf16[16,27,256]{2,0,1:T(8,128)(2,1)} %bitcast.67, bf16[16,27,128]{2,0,1:T(8,128)(2,1)} %bitcast.68), kind=kLoop, calls=%fused_computation.27 | loop fusion | flops 663552 | bytes 663552 | tf_op jit(solution)/shard_map/concatenate | solution.py:42
  8.3 0.0 all-gather.2.cloned.1.call-update
  8.3 3.5 %collective-permute-start = (bf16[2,8,4096]{2,1,0:T(8,128)(2,1)}, bf16[2,8,4096]{2,1,0:T(8,128)(2,1)S(1)}, u32[]{:S(2)}, u32[]{:S(2)}) collective-permute-start(bf16[2,8,4096]{2,1,0:T(8,128)(2,1)} %param.5), channel_id=1, source_target_pairs={{0,16},{16,32},{32,48},{48,64},{64,80},{80,96},{96,112},{112,128},... | collective-permute-start | bytes 393224 | tf_op jit(solution)/shard_map/ppermute | solution.py:33
  11.9 5.6 %collective-permute-start.1 = (bf16[2,8,4096]{2,1,0:T(8,128)(2,1)}, bf16[2,8,4096]{2,1,0:T(8,128)(2,1)S(1)}, u32[]{:S(2)}, u32[]{:S(2)}) collective-permute-start(bf16[2,8,4096]{2,1,0:T(8,128)(2,1)} %param.5), channel_id=1, source_target_pairs={{16,0},{32,16},{48,32},{64,48},{80,64},{96,80},{112,96},{128,112},... | collective-permute-start | bytes 393224 | tf_op jit(solution)/shard_map/ppermute | solution.py:34
  17.5 0.7 pad_maximum_fusion.4
  18.2 0.6 broadcast_in_dim.13
  18.8 6.9 %all-to-all-start.1 = ((f32[16,2,16]{2,1,0:T(2,128)}), f32[16,2,16]{2,1,0:T(2,128)S(1)}, u32[]{:S(2)}, u32[]{:S(2)}) async-start(f32[16,2,16]{2,1,0:T(2,128)} %broadcast_in_dim.13), calls=%async_computation.1 | async-start | bytes 32768 | tf_op jit(solution)/shard_map/all_to_all | solution.py:54
  25.7 0.0 collective-permute-done
  25.7 0.0 collective-permute-done.1
  25.7 1.0 %pad_maximum_fusion.2 = bf16[6,8,4096]{2,1,0:T(8,128)(2,1)S(1)} fusion(bf16[2,8,4096]{2,1,0:T(8,128)(2,1)S(1)} %collective-permute-done.1, bf16[2,8,4096]{2,1,0:T(8,128)(2,1)} %param.5, bf16[2,8,4096]{2,1,0:T(8,128)(2,1)S(1)} %collective-permute-done), kind=kLoop, calls=%fused_computation.26 | loop fusion | flops 393216 | bytes 786432 | tf_op jit(solution)/shard_map/concatenate | solution.py:35
  26.7 0.8 reshape.83
  27.5 0.7 pad_slice_fusion.1
  28.2 0.5 copy.41
  28.7 0.5 copy.42
  29.2 0.3 pad_maximum_fusion
  29.6 0.5 copy.54
  30.0 1.7 %reshape.112 = bf16[6,8,16,512]{3,1,0,2:T(8,128)(2,1)} reshape(bf16[6,8,16,8,64]{4,3,1,0,2:T(8,128)(2,1)S(1)} %copy.54) | data formatting | bytes 1572864 | tf_op jit(solution)/shard_map/reshape | solution.py:79
  31.7 0.0 all-to-all-done.1
  31.7 5.7 %all-to-all-start = ((bf16[6,8,16,512]{3,1,0,2:T(8,128)(2,1)}), bf16[6,8,16,512]{3,1,0,2:T(8,128)(2,1)S(1)}, u32[]{:S(2)}, u32[]{:S(2)}) async-start(bf16[6,8,16,512]{3,1,0,2:T(8,128)(2,1)} %reshape.112), calls=%async_computation | async-start | bytes 1572864 | tf_op jit(solution)/shard_map/all_to_all | solution.py:80
  37.5 0.1 broadcast_and_fusion
  37.6 0.1 add.50
  37.7 18.9 %all-to-all-done = bf16[6,8,16,512]{3,1,0,2:T(8,128)(2,1)S(1)} async-done(((bf16[6,8,16,512]{3,1,0,2:T(8,128)(2,1)}), bf16[6,8,16,512]{3,1,0,2:T(8,128)(2,1)S(1)}, u32[]{:S(2)}, u32[]{:S(2)}) %all-to-all-start) | async-done | bytes 786464 | tf_op jit(solution)/shard_map/all_to_all | solution.py:80
  56.6 0.1 copy.45
  56.6 0.8 reshape.106
  57.5 1.1 %copy.56 = bf16[6,128,8,1,64]{1,2,4,0,3:T(8,128)(2,1)S(1)} copy(bf16[6,128,8,1,64]{4,2,1,0,3:T(8,128)(2,1)S(1)} %reshape.106) | data formatting | bytes 1572864
  58.6 0.1 pad.5.clone
  58.7 0.1 copy.48
  58.8 0.1 slice.46
  58.9 0.0 copy-start
  58.9 3.4 %all-gather.2.cloned.1.call-done = bf16[256,27,384]{2,0,1:T(8,128)(2,1)} async-done(((bf16[16,27,384]{2,0,1:T(8,128)(2,1)}), bf16[256,27,384]{2,0,1:T(8,128)(2,1)}) %all-gather.2.cloned.1.call-update) | async-done | bytes 5308432 | tf_op jit(solution)/shard_map/all_gather | solution.py:42
  62.3 0.0 copy-done
  62.3 1.5 %slice-done.2 = bf16[256,27,128]{2,0,1:T(8,128)(2,1)S(1)} async-done(((bf16[256,27,384]{2,0,1:T(8,128)(2,1)}), bf16[256,27,128]{2,0,1:T(8,128)(2,1)S(1)}, s32[]{:S(2)}) %slice-start.2) | async-done | bytes 1769496 | tf_op jit(solution)/shard_map/slice | solution.py:45
  63.8 3.7 %fusion.6 = bf16[4,6,1,8,9,256]{5,3,4,1,0,2:T(8,128)(2,1)S(1)} fusion(bf16[256,3,3,3,128]{4,0,3,2,1:T(8,128)(2,1)S(1)} %bitcast.57, bf16[6,128,8,1,7,2]{1,4,5,2,0,3:T(8,128)(2,1)S(1)} %slice.46, bf16[6,128,8,1,8,9]{1,4,5,2,0,3:T(8,128)(2,1)S(1)} %copy.48, f32[256]{0:T(256)S(1)} %add.50, pred[8,9]{0,1:T(8,128)(4,1)S(1)} %copy-done, ...), kind=kOutput, calls=%fused_computation.12 | convolution fusion | flops 3064430592 | bytes 3712096 | tf_op jit(solution)/shard_map/conv_general_dilated | solution.py:18
  67.5 0.0 slice-done
  67.6 0.0 slice-done.1
  67.6 0.3 fusion.25
  67.9 2.2 %fusion.23 = f32[2,4,8,9,128]{4,2,3,1,0:T(8,128)S(1)} fusion(bf16[128,3,3,3,256]{4,0,3,2,1:T(8,128)(2,1)S(1)} %bitcast.63, bf16[4,6,1,7,1,256]{5,3,4,1,0,2:T(8,128)(2,1)S(1)} %get-tuple-element.8, bf16[4,6,1,7,1,256]{5,3,4,1,0,2:T(8,128)(2,1)S(1)} %get-tuple-element.7, bf16[4,6,1,8,9,256]{5,3,4,1,0,2:T(8,128)(2,1)S(1)} %fusion.6), kind=kOutput, calls=%fused_computation.39 | convolution fusion | flops 1024622592 | bytes 3121152 | tf_op jit(solution)/shard_map/conv_general_dilated | solution.py:18
  70.1 0.1 copy.49
  70.2 2.2 %fusion.21 = f32[2,4,8,9,128]{4,2,3,1,0:T(8,128)S(1)} fusion(bf16[128,3,3,3,256]{4,0,3,2,1:T(8,128)(2,1)S(1)} %bitcast.62, bf16[4,6,1,7,1,256]{5,3,4,1,0,2:T(8,128)(2,1)S(1)} %get-tuple-element.8, bf16[4,6,1,7,1,256]{5,3,4,1,0,2:T(8,128)(2,1)S(1)} %get-tuple-element.7, bf16[4,6,1,8,9,256]{5,3,4,1,0,2:T(8,128)(2,1)S(1)} %fusion.6), kind=kOutput, calls=%fused_computation.38 | convolution fusion | flops 1024622592 | bytes 3121152 | tf_op jit(solution)/shard_map/conv_general_dilated | solution.py:18
  72.4 0.1 copy.50
  72.6 0.1 pad_maximum_fusion.1
  72.7 0.4 copy.51
  73.1 0.6 concatenate.18
  73.7 0.1 fusion.17
  73.9 11.2 %all_to_all.35 = bf16[2,16,16,256]{3,2,0,1:T(8,128)(2,1)S(1)} all-to-all(bf16[2,16,16,256]{3,2,0,1:T(8,128)(2,1)S(1)} %copy.52), channel_id=1, replica_groups=mesh['depth'=16,'filt'=16] {'filt'}, dimensions={1} | all-to-all | bytes 524288 | tf_op jit(solution)/shard_map/all_to_all | solution.py:92
  85.1 0.1 copy.53
  85.3 0.8 reshape.90
  (10 shorter events, 0.1 us)
Async XLA Ops:
  6.5 55.8 %all-gather.2.cloned.1.call-start = ((), (), s32[]{:S(2)}) async-start(), calls=%async_computation.3 | async-start | bytes 5640192 | tf_op jit(solution)/shard_map/all_gather | solution.py:42
  8.3 17.4 %collective-permute-start = (bf16[2,8,4096]{2,1,0:T(8,128)(2,1)}, bf16[2,8,4096]{2,1,0:T(8,128)(2,1)S(1)}, u32[]{:S(2)}, u32[]{:S(2)}) collective-permute-start(bf16[2,8,4096]{2,1,0:T(8,128)(2,1)} %param.5), channel_id=1, source_target_pairs={{0,16},{16,32},{32,48},{48,64},{64,80},{80,96},{96,112},{112,128},... | collective-permute-start | bytes 393224 | tf_op jit(solution)/shard_map/ppermute | solution.py:33
  11.9 13.8 %collective-permute-start.1 = (bf16[2,8,4096]{2,1,0:T(8,128)(2,1)}, bf16[2,8,4096]{2,1,0:T(8,128)(2,1)S(1)}, u32[]{:S(2)}, u32[]{:S(2)}) collective-permute-start(bf16[2,8,4096]{2,1,0:T(8,128)(2,1)} %param.5), channel_id=1, source_target_pairs={{16,0},{32,16},{48,32},{64,48},{80,64},{96,80},{112,96},{128,112},... | collective-permute-start | bytes 393224 | tf_op jit(solution)/shard_map/ppermute | solution.py:34
  18.8 12.9 %all-to-all-start.1 = ((f32[16,2,16]{2,1,0:T(2,128)}), f32[16,2,16]{2,1,0:T(2,128)S(1)}, u32[]{:S(2)}, u32[]{:S(2)}) async-start(f32[16,2,16]{2,1,0:T(2,128)} %broadcast_in_dim.13), calls=%async_computation.1 | async-start | bytes 32768 | tf_op jit(solution)/shard_map/all_to_all | solution.py:54
  31.7 24.8 %all-to-all-start = ((bf16[6,8,16,512]{3,1,0,2:T(8,128)(2,1)}), bf16[6,8,16,512]{3,1,0,2:T(8,128)(2,1)S(1)}, u32[]{:S(2)}, u32[]{:S(2)}) async-start(bf16[6,8,16,512]{3,1,0,2:T(8,128)(2,1)} %reshape.112), calls=%async_computation | async-start | bytes 1572864 | tf_op jit(solution)/shard_map/all_to_all | solution.py:80
  58.9 3.4 %copy-start = (pred[8,9]{0,1:T(8,128)(4,1)S(1)}, pred[8,9]{0,1:T(8,128)(4,1)}, u32[]{:S(2)}) copy-start(pred[8,9]{0,1:T(8,128)(4,1)} %constant.45) | copy-start | bytes 220
  62.3 1.5 %slice-start.2 = ((bf16[256,27,384]{2,0,1:T(8,128)(2,1)}), bf16[256,27,128]{2,0,1:T(8,128)(2,1)S(1)}, s32[]{:S(2)}) async-start(bf16[256,27,384]{2,0,1:T(8,128)(2,1)} %all-gather.2.cloned.1.call-done), calls=%async_computation.6 | async-start | bytes 3538944 | tf_op jit(solution)/shard_map/slice | solution.py:45
  62.3 5.3 %slice-start = ((s8[5308416]{0:T(1024)(128)(4,1)}), s8[4194304]{0:T(1024)(128)(4,1)S(1)}, s32[]{:S(2)}) async-start(s8[5308416]{0:T(1024)(128)(4,1)} %bitcast.55), calls=%async_computation.4 | async-start | bytes 8388608
  63.8 3.8 %slice-start.1 = ((s8[5308416]{0:T(1024)(128)(4,1)}), s8[1114112]{0:T(1024)(128)(4,1)S(1)}, s32[]{:S(2)}) async-start(s8[5308416]{0:T(1024)(128)(4,1)} %bitcast.55), calls=%async_computation.5 | async-start | bytes 2228224
Sparse Core Ops, SparseCore 0:
  9.2 53.0 all-gather.1

commit v6 on v2

--- a/solution.py
+++ b/solution.py
@@ -80,7 +80,18 @@
     mine = lax.all_to_all(windows, "filt", 2, 1, tiled=True)
     mine = mine.reshape(planes + 4, count * chans, block_rows + 4, SIDE)
 
-    hidden = activate(conv(mine, kernel_1), bias_1)
+    count_out = planes + 2
+    stacked = jnp.concatenate([mine[i : i + count_out] for i in range(3)], axis=1)
+    taps_1 = jnp.transpose(kernel_1, (0, 2, 3, 1, 4)).reshape(kernel_1.shape[0], 3, 3, 3 * kernel_1.shape[4])
+    summed_1 = lax.conv_general_dilated(
+        stacked,
+        taps_1,
+        (1, 1),
+        ((0, 0), (1, 1)),
+        dimension_numbers=("NCHW", "OHWI", "NCHW"),
+        preferred_element_type=jnp.float32,
+    )
+    hidden = activate(summed_1, bias_1)
     grid = inside(planes * lax.axis_size("depth"), rows, planes, block_rows)
     hidden = jnp.where(grid, hidden, jnp.zeros_like(hidden))
     second = activate(conv(hidden, kernel_2), bias_2)

time: 94.1 us -> 106 us (1.13)
  local copies, waits for them, and re-layouts: 13.4 us -> 22.9 us
  other arithmetic: 3.95 us -> 7.78 us
  waiting for transfers between devices: 22.3 us -> 18.9 us
  matrix products: 6.06 us -> 7.71 us
  blocking collectives: 11.2 us -> 12.4 us
    conv_general_dilated x0 -> x1, matrix products: none -> 5.43 us  [local(): lax.conv_general_dilated(stacked, taps_1, (1, 1), ((0, 0), (1, 1)), dimen...]
    slice x0 -> x7, local copies, waits for them, and re-layouts: none -> 4.89 us  [local(): stacked = jnp.concatenate([mine[i:i + count_out] for i in range(3)], axis=1)]
    conv_general_dilated x2 -> x1, matrix products: 6.06 us -> 2.28 us  [conv(): lax.conv_general_dilated(framed[None], kernel, (1, 1, 1), ((0, 0), (0, 0)...]
    all_gather x1, waiting for transfers between devices: 3.42 us -> 0.01 us  [gather_kernels(): lax.all_gather(jnp.concatenate([first, second], axis=2), 'filt', axis=0,...]
    concatenate x0 -> x1, other arithmetic: none -> 2.19 us  [local(): stacked = jnp.concatenate([mine[i:i + count_out] for i in range(3)], axis=1)]
    unnamed x3, local copies, waits for them, and re-layouts: 1.12 us -> 3.09 us
    conv_general_dilated x0 -> x1, other arithmetic: none -> 1.62 us  [local(): lax.conv_general_dilated(stacked, taps_1, (1, 1), ((0, 0), (1, 1)), dimen...]
    concatenate x0 -> x1, local copies, waits for them, and re-layouts: none -> 1.57 us  [local(): stacked = jnp.concatenate([mine[i:i + count_out] for i in range(3)], axis=1)]
  transfers between devices with their start and end apart: 5 -> 5, of which waited for: 2 -> 1; matrix products, arithmetic and copies ran while one was open for 10% -> 20% of each run, Pallas kernels for 0% -> 0%
where the time goes in v6:
time: 106 us; the launch traced here: 105 us
  local copies, waits for them, and re-layouts  22.9 us (22%)
  starting transfers between devices  21.8 us (21%)
  waiting for transfers between devices  18.9 us (18%)
  between operations  13.7 us (13%)
  blocking collectives  12.4 us (12%)
  other arithmetic  7.78 us (7%)
  matrix products  7.71 us (7%)
    all_to_all x1, waiting for transfers between devices, local(): mine = lax.all_to_all(windows, 'filt', 2, 1, tiled=True)  18.9 us
    all_to_all x1, blocking collectives, local(): result = lax.all_to_all(second, 'filt', 1, 3, tiled=True)  12.4 us
    all_to_all x1, starting transfers between devices, gather_biases(): whole = lax.all_to_all(spread, 'filt', 0, 0, tiled=True)  6.88 us
    all_to_all x1, starting transfers between devices, local(): mine = lax.all_to_all(windows, 'filt', 2, 1, tiled=True)  5.72 us
    ppermute x1, starting transfers between devices, depth_halo(): high = lax.ppermute(block[:reach], 'depth', backward)  5.63 us
    conv_general_dilated x1, matrix products, local(): lax.conv_general_dilated(stacked, taps_1, (1, 1), ((0, 0), (1, 1)), dimen...  5.43 us
    slice x7, local copies, waits for them, and re-layouts, local(): stacked = jnp.concatenate([mine[i:i + count_out] for i in range(3)], axis=1)  4.89 us
    ppermute x1, starting transfers between devices, depth_halo(): low = lax.ppermute(block[block.shape[0] - reach:], 'depth', forward)  3.55 us
  transfers between devices with their start and end apart: 5, of which 1 were waited for; matrix products, arithmetic and copies ran while one was open for 20% of the time, Pallas kernels for 0%

profile of v6, /device:TPU:17, one launch (start us, length us, event | category | flops | bytes accessed | tf_op | source)
XLA Modules:
  0.0 105.1 jit_solution(3945171308036549280)
XLA Ops:
  6.5 1.8 %pad_maximum_fusion.2 = bf16[16,27,384]{2,0,1:T(8,128)(2,1)} fusion(bf16[16,27,256]{2,0,1:T(8,128)(2,1)} %bitcast.82, bf16[16,27,128]{2,0,1:T(8,128)(2,1)} %bitcast.83), kind=kLoop, calls=%fused_computation.27 | loop fusion | flops 663552 | bytes 663552 | tf_op jit(solution)/shard_map/concatenate | solution.py:42
  8.3 0.0 all-gather.2.cloned.1.call-update
  8.4 3.5 %collective-permute-start = (bf16[2,8,4096]{2,1,0:T(8,128)(2,1)}, bf16[2,8,4096]{2,1,0:T(8,128)(2,1)S(1)}, u32[]{:S(2)}, u32[]{:S(2)}) collective-permute-start(bf16[2,8,4096]{2,1,0:T(8,128)(2,1)} %param.5), channel_id=1, source_target_pairs={{0,16},{16,32},{32,48},{48,64},{64,80},{80,96},{96,112},{112,128},... | collective-permute-start | bytes 393224 | tf_op jit(solution)/shard_map/ppermute | solution.py:33
  11.9 5.6 %collective-permute-start.1 = (bf16[2,8,4096]{2,1,0:T(8,128)(2,1)}, bf16[2,8,4096]{2,1,0:T(8,128)(2,1)S(1)}, u32[]{:S(2)}, u32[]{:S(2)}) collective-permute-start(bf16[2,8,4096]{2,1,0:T(8,128)(2,1)} %param.5), channel_id=1, source_target_pairs={{16,0},{32,16},{48,32},{64,48},{80,64},{96,80},{112,96},{128,112},... | collective-permute-start | bytes 393224 | tf_op jit(solution)/shard_map/ppermute | solution.py:34
  17.6 0.7 pad_maximum_fusion.3
  18.2 0.6 broadcast_in_dim.23
  18.9 6.9 %all-to-all-start.1 = ((f32[16,2,16]{2,1,0:T(2,128)}), f32[16,2,16]{2,1,0:T(2,128)S(1)}, u32[]{:S(2)}, u32[]{:S(2)}) async-start(f32[16,2,16]{2,1,0:T(2,128)} %broadcast_in_dim.23), calls=%async_computation.1 | async-start | bytes 32768 | tf_op jit(solution)/shard_map/all_to_all | solution.py:54
  25.7 0.0 collective-permute-done
  25.7 0.0 collective-permute-done.1
  25.8 1.0 pad_maximum_fusion.1
  26.7 0.8 reshape.90
  27.6 0.7 pad_slice_fusion.1
  28.2 0.5 copy.62
  28.7 0.5 copy.63
  29.3 0.3 pad_maximum_fusion
  29.6 0.5 copy.81
  30.1 1.7 %reshape.123 = bf16[6,8,16,512]{3,1,0,2:T(8,128)(2,1)} reshape(bf16[6,8,16,8,64]{4,3,1,0,2:T(8,128)(2,1)S(1)} %copy.81) | data formatting | bytes 1572864 | tf_op jit(solution)/shard_map/reshape | solution.py:79
  31.8 0.0 all-to-all-done.1
  31.8 5.7 %all-to-all-start = ((bf16[6,8,16,512]{3,1,0,2:T(8,128)(2,1)}), bf16[6,8,16,512]{3,1,0,2:T(8,128)(2,1)S(1)}, u32[]{:S(2)}, u32[]{:S(2)}) async-start(bf16[6,8,16,512]{3,1,0,2:T(8,128)(2,1)} %reshape.123), calls=%async_computation | async-start | bytes 1572864 | tf_op jit(solution)/shard_map/all_to_all | solution.py:80
  37.5 0.1 and_bitcast_fusion
  37.6 0.1 add.49
  37.7 18.9 %all-to-all-done = bf16[6,8,16,512]{3,1,0,2:T(8,128)(2,1)S(1)} async-done(((bf16[6,8,16,512]{3,1,0,2:T(8,128)(2,1)}), bf16[6,8,16,512]{3,1,0,2:T(8,128)(2,1)S(1)}, u32[]{:S(2)}, u32[]{:S(2)}) %all-to-all-start) | async-done | bytes 786464 | tf_op jit(solution)/shard_map/all_to_all | solution.py:80
  56.6 0.1 fusion.22
  56.7 1.6 %slice.39 = bf16[4,128,8,64]{3,2,1,0:T(8,128)(2,1)} reshape(bf16[4,16,8,1,512]{4,2,1,0,3:T(8,128)(2,1)S(1)} %copy.66) | data formatting | bytes 1048576 | tf_op jit(solution)/shard_map/slice | solution.py:84
  58.4 1.5 %slice.41 = bf16[4,128,8,64]{3,2,1,0:T(8,128)(2,1)} reshape(bf16[4,16,8,1,512]{4,2,1,0,3:T(8,128)(2,1)S(1)} %copy.67) | data formatting | bytes 1048576 | tf_op jit(solution)/shard_map/slice | solution.py:84
  59.9 1.6 %slice.43 = bf16[4,128,8,64]{3,2,1,0:T(8,128)(2,1)} reshape(bf16[4,16,8,1,512]{4,2,1,0,3:T(8,128)(2,1)S(1)} %copy.68) | data formatting | bytes 1048576 | tf_op jit(solution)/shard_map/slice | solution.py:84
  61.5 2.2 %maximum_bitcast_fusion = bf16[384,8,4,64]{3,1,0,2:T(8,128)(2,1)S(1)} fusion(bf16[4,128,8,64]{3,2,1,0:T(8,128)(2,1)} %slice.43, bf16[4,128,8,64]{3,2,1,0:T(8,128)(2,1)} %slice.41, bf16[4,128,8,64]{3,2,1,0:T(8,128)(2,1)} %slice.39), kind=kLoop, calls=%fused_computation.3 | loop fusion | flops 1572864 | bytes 3145728 | tf_op jit(solution)/shard_map/concatenate | solution.py:84
  63.7 3.1 %copy.85 = bf16[384,8,4,64]{0,1,3,2:T(8,128)(2,1)} copy(bf16[384,8,4,64]{3,1,0,2:T(8,128)(2,1)S(1)} %maximum_bitcast_fusion) | data formatting | bytes 3145728
  66.8 1.6 %pad.5.clone = bf16[384,8,4,72]{0,1,3,2:T(8,128)(2,1)S(1)} pad(bf16[384,8,4,64]{0,1,3,2:T(8,128)(2,1)} %copy.85, bf16[]{:T(256)} %constant.10.clone.1), padding=0_0x0_0x0_0x1_7 | pad | bytes 3342338 | tf_op jit(solution)/shard_map/concatenate | solution.py:84
  68.4 1.6 %fusion.1 = bf16[384,8,4,8,11]{0,1,4,3,2:T(8,128)(2,1)} fusion(bf16[384,8,4,7,2]{0,1,4,3,2:T(8,128)(2,1)S(1)} %slice.55, bf16[384,8,4,8,9]{0,1,4,3,2:T(8,128)(2,1)S(1)} %bitcast.70), kind=kLoop, calls=%fused_computation.4 | loop fusion | flops 6488064 | bytes 4276224 | tf_op jit(solution)/shard_map/conv_general_dilated | solution.py:86
  70.0 1.5 %slice-done = bf16[256,27,128]{2,0,1:T(8,128)(2,1)S(1)} async-done(((bf16[256,27,384]{2,0,1:T(8,128)(2,1)}), bf16[256,27,128]{2,0,1:T(8,128)(2,1)S(1)}, s32[]{:S(2)}) %slice-start) | async-done | bytes 1769496 | tf_op jit(solution)/shard_map/slice | solution.py:45
  71.5 0.9 copy.71
  72.4 0.2 broadcast.73
  72.6 5.4 %copy_select_fusion = bf16[6,32,9,256]{3,1,2,0:T(8,128)(2,1)S(1)} fusion(pred[6,32,9,256]{3,0,2,1:T(8,128)(4,1)S(1)} %bitcast.81, bf16[256,3,3,384]{0,3,2,1:T(8,128)(2,1)S(1)} %bitcast.79, bf16[384,8,4,8,11]{0,1,4,3,2:T(8,128)(2,1)} %fusion.1, f32[256]{0:T(256)S(1)} %add.49, pred[32,9]{0,1:T(8,128)(4,1)} %constant.44), kind=kOutput, calls=%fused_computation.11 | convolution fusion | flops 3060744192 | bytes 5260576 | tf_op jit(solution)/shard_map/conv_general_dilated | solution.py:86
  78.1 0.5 copy.73
  78.6 0.1 slice_bitcast_fusion
  78.6 0.2 pad.7
  78.9 0.2 copy.76
  79.1 0.0 copy-start
  79.1 2.0 %slice-done.1 = bf16[256,27,256]{2,0,1:T(8,128)(2,1)S(1)} async-done(((bf16[256,27,384]{2,0,1:T(8,128)(2,1)}), bf16[256,27,256]{2,0,1:T(8,128)(2,1)S(1)}, s32[]{:S(2)}) %slice-start.1) | async-done | bytes 3538968 | tf_op jit(solution)/shard_map/slice | solution.py:46
  81.1 2.3 %convolution_select_fusion = f32[2,4,8,9,256]{4,2,3,1,0:T(8,128)S(1)} fusion(bf16[256,3,3,3,256]{4,0,3,2,1:T(8,128)(2,1)S(1)} %bitcast.72, bf16[4,256,6,1,7,2]{1,4,5,2,0,3:T(8,128)(2,1)S(1)} %slice.59, bf16[4,256,6,1,8,9]{1,4,5,2,0,3:T(8,128)(2,1)S(1)} %copy.76, pred[8,9]{0,1:T(8,128)(4,1)S(1)} %copy-done), kind=kOutput, calls=%fused_computation.14 | convolution fusion | flops 2041823232 | bytes 5185608 | tf_op jit(solution)/shard_map/conv_general_dilated | solution.py:18
  83.4 0.2 copy.77
  83.7 0.4 copy.78
  84.1 0.6 squeeze.3
  84.7 0.1 fusion.18
  84.9 12.4 %all_to_all.35 = bf16[2,16,16,256]{3,2,0,1:T(8,128)(2,1)S(1)} all-to-all(bf16[2,16,16,256]{3,2,0,1:T(8,128)(2,1)S(1)} %copy.79), channel_id=1, replica_groups=mesh['depth'=16,'filt'=16] {'filt'}, dimensions={1} | all-to-all | bytes 524288 | tf_op jit(solution)/shard_map/all_to_all | solution.py:101
  97.3 0.1 copy.80
  97.5 0.8 reshape.99
  (15 shorter events, 0.3 us)
Async XLA Ops:
  6.5 63.5 %all-gather.2.cloned.1.call-start = ((), (), s32[]{:S(2)}) async-start(), calls=%async_computation.3 | async-start | bytes 5640192 | tf_op jit(solution)/shard_map/all_gather | solution.py:42
  8.4 17.4 %collective-permute-start = (bf16[2,8,4096]{2,1,0:T(8,128)(2,1)}, bf16[2,8,4096]{2,1,0:T(8,128)(2,1)S(1)}, u32[]{:S(2)}, u32[]{:S(2)}) collective-permute-start(bf16[2,8,4096]{2,1,0:T(8,128)(2,1)} %param.5), channel_id=1, source_target_pairs={{0,16},{16,32},{32,48},{48,64},{64,80},{80,96},{96,112},{112,128},... | collective-permute-start | bytes 393224 | tf_op jit(solution)/shard_map/ppermute | solution.py:33
  11.9 13.8 %collective-permute-start.1 = (bf16[2,8,4096]{2,1,0:T(8,128)(2,1)}, bf16[2,8,4096]{2,1,0:T(8,128)(2,1)S(1)}, u32[]{:S(2)}, u32[]{:S(2)}) collective-permute-start(bf16[2,8,4096]{2,1,0:T(8,128)(2,1)} %param.5), channel_id=1, source_target_pairs={{16,0},{32,16},{48,32},{64,48},{80,64},{96,80},{112,96},{128,112},... | collective-permute-start | bytes 393224 | tf_op jit(solution)/shard_map/ppermute | solution.py:34
  18.9 12.9 %all-to-all-start.1 = ((f32[16,2,16]{2,1,0:T(2,128)}), f32[16,2,16]{2,1,0:T(2,128)S(1)}, u32[]{:S(2)}, u32[]{:S(2)}) async-start(f32[16,2,16]{2,1,0:T(2,128)} %broadcast_in_dim.23), calls=%async_computation.1 | async-start | bytes 32768 | tf_op jit(solution)/shard_map/all_to_all | solution.py:54
  31.8 24.8 %all-to-all-start = ((bf16[6,8,16,512]{3,1,0,2:T(8,128)(2,1)}), bf16[6,8,16,512]{3,1,0,2:T(8,128)(2,1)S(1)}, u32[]{:S(2)}, u32[]{:S(2)}) async-start(bf16[6,8,16,512]{3,1,0,2:T(8,128)(2,1)} %reshape.123), calls=%async_computation | async-start | bytes 1572864 | tf_op jit(solution)/shard_map/all_to_all | solution.py:80
  70.0 1.5 %slice-start = ((bf16[256,27,384]{2,0,1:T(8,128)(2,1)}), bf16[256,27,128]{2,0,1:T(8,128)(2,1)S(1)}, s32[]{:S(2)}) async-start(bf16[256,27,384]{2,0,1:T(8,128)(2,1)} %all-gather.2.cloned.1.call-done), calls=%async_computation.4 | async-start | bytes 3538944 | tf_op jit(solution)/shard_map/slice | solution.py:45
  79.1 2.0 %slice-start.1 = ((bf16[256,27,384]{2,0,1:T(8,128)(2,1)}), bf16[256,27,256]{2,0,1:T(8,128)(2,1)S(1)}, s32[]{:S(2)}) async-start(bf16[256,27,384]{2,0,1:T(8,128)(2,1)} %all-gather.2.cloned.1.call-done), calls=%async_computation.5 | async-start | bytes 7077888 | tf_op jit(solution)/shard_map/slice | solution.py:46
  79.1 2.0 %copy-start = (pred[8,9]{0,1:T(8,128)(4,1)S(1)}, pred[8,9]{0,1:T(8,128)(4,1)}, u32[]{:S(2)}) copy-start(pred[8,9]{0,1:T(8,128)(4,1)} %constant.43) | copy-start | bytes 220
Sparse Core Ops, SparseCore 0:
  9.2 53.0 all-gather.1

commit v7 on v2

--- a/solution.py
+++ b/solution.py
@@ -47,11 +47,20 @@
     )
 
 
-def gather_biases(first_bias, second_bias):
-    count = lax.axis_size("filt")
-    pair = jnp.stack([first_bias, second_bias])
-    spread = jnp.broadcast_to(pair[None], (count,) + pair.shape)
-    whole = lax.all_to_all(spread, "filt", 0, 0, tiled=True)
+def bias_parts(first_bias, second_bias):
+    parts = []
+    for bias in (first_bias, second_bias):
+        rest = bias
+        for _ in range(3):
+            piece = rest.astype(jnp.bfloat16)
+            parts.append(piece)
+            rest = rest - piece.astype(jnp.float32)
+    return jnp.stack(parts).reshape(-1)
+
+
+def joined_biases(received, outs):
+    parts = received.astype(jnp.float32).reshape(received.shape[0], 2, 3, outs)
+    whole = (parts[:, :, 0] + parts[:, :, 1]) + parts[:, :, 2]
     return whole[:, 0].reshape(-1), whole[:, 1].reshape(-1)
 
 
@@ -69,16 +78,21 @@
     rows = cells // SIDE
     block_rows = rows // count
     kernel_1, kernel_2 = gather_kernels(first_kernel, second_kernel)
-    bias_1, bias_2 = gather_biases(first_bias, second_bias)
 
     extended = depth_halo(features, 2).reshape(planes + 4, chans, rows, SIDE)
     framed = jnp.pad(extended, ((0, 0), (0, 0), (2, max(2, block_rows)), (0, 0)))
     heads = framed[:, :, :rows].reshape(planes + 4, chans, count, block_rows, SIDE)
     tails = framed[:, :, block_rows : rows + block_rows].reshape(planes + 4, chans, count, block_rows, SIDE)
     windows = jnp.concatenate([heads, tails[:, :, :, : 4]], axis=3)
-    windows = windows.reshape(planes + 4, chans, count, (block_rows + 4) * SIDE)
-    mine = lax.all_to_all(windows, "filt", 2, 1, tiled=True)
-    mine = mine.reshape(planes + 4, count * chans, block_rows + 4, SIDE)
+    span = (block_rows + 4) * SIDE
+    windows = windows.reshape(planes + 4, chans, count, span)
+    parts = bias_parts(first_bias, second_bias)
+    extra = jnp.zeros((planes + 4, 1, count, span), jnp.bfloat16)
+    extra = extra.at[0, 0, :, : parts.shape[0]].set(jnp.broadcast_to(parts, (count, parts.shape[0])))
+    sent = jnp.concatenate([windows, extra], axis=1)
+    got = lax.all_to_all(sent, "filt", 2, 1, tiled=True).reshape(planes + 4, count, chans + 1, span)
+    bias_1, bias_2 = joined_biases(got[0, :, chans, : parts.shape[0]], first_bias.shape[0])
+    mine = got[:, :, :chans].reshape(planes + 4, count * chans, block_rows + 4, SIDE)
 
     hidden = activate(conv(mine, kernel_1), bias_1)
     grid = inside(planes * lax.axis_size("depth"), rows, planes, block_rows)

time: 94.1 us -> 98.1 us (1.043); the launches traced: 92.4 us -> 97.5 us
  waiting for transfers between devices: 22.3 us -> 28.1 us
  starting transfers between devices: 21.8 us -> 16.7 us
  local copies, waits for them, and re-layouts: 13.4 us -> 16.7 us
  blocking collectives: 11.2 us -> 12.2 us
    all_to_all x2 -> x1, waiting for transfers between devices: 18.9 us -> 25.6 us  [local(): lax.all_to_all(sent, 'filt', 2, 1, tiled=True)]
    all_to_all x2 -> x1, starting transfers between devices: 12.6 us -> 7.48 us  [local(): lax.all_to_all(sent, 'filt', 2, 1, tiled=True)]
    all_gather x1, waiting for transfers between devices: 3.42 us -> 0.94 us  [gather_kernels(): lax.all_gather(jnp.concatenate([first, second], axis=2), 'filt', axis=0,...]
    concatenate x0 -> x2, local copies, waits for them, and re-layouts: none -> 1.96 us  [the longest x1 1.56 us: local(): sent = jnp.concatenate([windows, extra], axis=1)]
    another operation x2, local copies, waits for them, and re-layouts: 0.9 us -> 2.67 us  [conv(): framed[None]]
    reshape x2 -> x1, local copies, waits for them, and re-layouts: 2.16 us -> 0.96 us  [local(): windows = windows.reshape(planes + 4, chans, count, span)]
    slice x1 -> x2, local copies, waits for them, and re-layouts: 0.03 us -> 1.16 us  [the longest x1 1.13 us: local(): got[:, :, :chans].reshape(planes + 4, count * chans, block_rows + 4, SIDE)]
  transfers between devices with their start and end apart: 5 -> 4, of which waited for: 2 -> 4; matrix products, arithmetic and copies ran while one was open for 10% -> 14% of each run, Pallas kernels for 0% -> 0%
where the time goes in v7:
time: 98.1 us; the launch traced here: 97.5 us
  waiting for transfers between devices  28.1 us (29%)
  starting transfers between devices  16.7 us (17%)
  local copies, waits for them, and re-layouts  16.7 us (17%)
  between operations  13.6 us (14%)
  blocking collectives  12.2 us (12%)
  matrix products  6.05 us (6%)
  other arithmetic  4.16 us (4%)
    all_to_all x1, waiting for transfers between devices, local(): lax.all_to_all(sent, 'filt', 2, 1, tiled=True)  25.6 us
    all_to_all x1, blocking collectives, local(): result = lax.all_to_all(second, 'filt', 1, 3, tiled=True)  12.2 us
    all_to_all x1, starting transfers between devices, local(): lax.all_to_all(sent, 'filt', 2, 1, tiled=True)  7.48 us
    conv_general_dilated x2, matrix products, conv(): lax.conv_general_dilated(framed[None], kernel, (1, 1, 1), ((0, 0), (0, 0)...  6.05 us
    ppermute x1, starting transfers between devices, depth_halo(): high = lax.ppermute(block[:reach], 'depth', backward)  5.63 us
    ppermute x1, starting transfers between devices, depth_halo(): low = lax.ppermute(block[block.shape[0] - reach:], 'depth', forward)  3.55 us
    another operation x2, local copies, waits for them, and re-layouts, conv(): framed[None]  2.67 us
    slice x2, local copies, waits for them, and re-layouts, gather_kernels(): whole[:, :, chans:].reshape(total, 3, 3, 3, second_kernel.shape[4])  1.99 us
  transfers between devices with their start and end apart: 4, of which 4 were waited for; matrix products, arithmetic and copies ran while one was open for 14% of the time, Pallas kernels for 0%

profile of v7, /device:TPU:17, one launch (start us, length us, event | category | flops | bytes accessed | tf_op | source)
XLA Modules:
  0.0 97.5 jit_solution(4703248525096404157)
XLA Ops:
  6.5 0.0 all-gather.2.cloned.1.call-start
  6.5 1.8 %pad_maximum_fusion.3 = bf16[16,27,384]{2,0,1:T(8,128)(2,1)} fusion(bf16[16,27,256]{2,0,1:T(8,128)(2,1)} %bitcast.63, bf16[16,27,128]{2,0,1:T(8,128)(2,1)} %bitcast.64), kind=kLoop, calls=%fused_computation.35 | loop fusion | flops 663552 | bytes 663552 | tf_op jit(solution)/shard_map/concatenate | solution.py:42
  8.3 0.0 all-gather.2.cloned.1.call-update
  8.4 3.5 %collective-permute-start = (bf16[2,8,4096]{2,1,0:T(8,128)(2,1)}, bf16[2,8,4096]{2,1,0:T(8,128)(2,1)S(1)}, u32[]{:S(2)}, u32[]{:S(2)}) collective-permute-start(bf16[2,8,4096]{2,1,0:T(8,128)(2,1)} %param.7), channel_id=1, source_target_pairs={{0,16},{16,32},{32,48},{48,64},{64,80},{80,96},{96,112},{112,128},... | collective-permute-start | bytes 393224 | tf_op jit(solution)/shard_map/ppermute | solution.py:33
  11.9 5.6 %collective-permute-start.1 = (bf16[2,8,4096]{2,1,0:T(8,128)(2,1)}, bf16[2,8,4096]{2,1,0:T(8,128)(2,1)S(1)}, u32[]{:S(2)}, u32[]{:S(2)}) collective-permute-start(bf16[2,8,4096]{2,1,0:T(8,128)(2,1)} %param.7), channel_id=1, source_target_pairs={{16,0},{32,16},{48,32},{64,48},{80,64},{96,80},{112,96},{128,112},... | collective-permute-start | bytes 393224 | tf_op jit(solution)/shard_map/ppermute | solution.py:34
  17.6 0.7 convert_bitcast_fusion
  18.3 0.1 reshape.143
  18.4 0.6 collective-permute-done
  19.0 1.0 collective-permute-done.1
  20.0 0.9 pad_maximum_fusion.2
  21.0 0.8 reshape.139
  21.8 0.7 pad_slice_fusion.1
  22.5 0.5 copy.47
  23.0 0.5 copy.48
  23.5 0.3 pad_maximum_fusion
  23.8 0.4 copy.49
  24.2 1.0 reshape.142
  25.2 0.1 pad_maximum_fusion.1
  25.3 1.6 %copy.50 = bf16[6,9,16,512]{3,0,1,2:T(8,128)(2,1)} copy(bf16[6,9,16,512]{3,2,1,0:T(8,128)(2,1)S(1)} %pad_maximum_fusion.1) | data formatting | bytes 1769472 | tf_op jit(solution)/shard_map/concatenate | solution.py:92
  26.9 7.5 %all-to-all-start = ((bf16[6,9,16,512]{3,0,1,2:T(8,128)(2,1)}), bf16[6,9,16,512]{3,0,1,2:T(8,128)(2,1)S(1)}, u32[]{:S(2)}, u32[]{:S(2)}) async-start(bf16[6,9,16,512]{3,0,1,2:T(8,128)(2,1)} %copy.50), calls=%async_computation | async-start | bytes 2359296 | tf_op jit(solution)/shard_map/all_to_all | solution.py:93
  34.4 0.1 broadcast_and_fusion
  34.5 25.6 %all-to-all-done = bf16[6,9,16,512]{3,0,1,2:T(8,128)(2,1)S(1)} async-done(((bf16[6,9,16,512]{3,0,1,2:T(8,128)(2,1)}), bf16[6,9,16,512]{3,0,1,2:T(8,128)(2,1)S(1)}, u32[]{:S(2)}, u32[]{:S(2)}) %all-to-all-start) | async-done | bytes 884768 | tf_op jit(solution)/shard_map/all_to_all | solution.py:93
  60.0 1.1 %slice.76 = bf16[6,16,8,512]{3,0,2,1:T(8,128)(2,1)} slice(bf16[6,16,9,512]{3,0,2,1:T(8,128)(2,1)S(1)} %bitcast.56), slice={[0:6], [0:16], [0:8], [0:512]} | slice | bytes 1572864 | tf_op jit(solution)/shard_map/slice | solution.py:95
  61.2 2.6 %reshape.166 = bf16[6,128,8,1,64]{4,2,0,1,3:T(8,128)(2,1)S(1)} reshape(bf16[6,16,8,512]{3,0,2,1:T(8,128)(2,1)} %slice.76) | data formatting | bytes 1572864 | tf_op jit(solution)/shard_map/broadcast_in_dim;reshape | solution.py:19
  63.8 1.2 %copy.59 = bf16[6,128,8,1,64]{1,2,4,0,3:T(8,128)(2,1)S(1)} copy(bf16[6,128,8,1,64]{4,2,0,1,3:T(8,128)(2,1)S(1)} %reshape.166) | data formatting | bytes 1572864
  65.0 0.1 pad.10.clone
  65.1 0.1 copy.54
  65.2 0.1 slice.77
  65.3 0.1 reshape.160
  65.4 0.1 add.67
  65.5 0.0 copy-start
  65.5 0.9 all-gather.2.cloned.1.call-done
  66.5 0.0 slice-start
  66.5 0.0 copy-done
  66.5 1.5 %slice-done = bf16[256,27,128]{2,0,1:T(8,128)(2,1)S(1)} async-done(((bf16[256,27,384]{2,0,1:T(8,128)(2,1)}), bf16[256,27,128]{2,0,1:T(8,128)(2,1)S(1)}, s32[]{:S(2)}) %slice-start) | async-done | bytes 1769496 | tf_op jit(solution)/shard_map/slice | solution.py:45
  68.0 3.7 %fusion.6 = bf16[4,6,1,8,9,256]{5,3,4,1,0,2:T(8,128)(2,1)S(1)} fusion(bf16[256,3,3,3,128]{4,0,3,2,1:T(8,128)(2,1)S(1)} %bitcast.54, bf16[6,128,8,1,7,2]{1,4,5,2,0,3:T(8,128)(2,1)S(1)} %slice.77, bf16[6,128,8,1,8,9]{1,4,5,2,0,3:T(8,128)(2,1)S(1)} %copy.54, f32[256]{0:T(256)S(1)} %add.67, pred[8,9]{0,1:T(8,128)(4,1)S(1)} %copy-done, ...), kind=kOutput, calls=%fused_computation.12 | convolution fusion | flops 3064430592 | bytes 3712096 | tf_op jit(solution)/shard_map/conv_general_dilated | solution.py:18
  71.7 0.0 slice-start.1
  71.8 2.0 %slice-done.1 = bf16[256,27,256]{2,0,1:T(8,128)(2,1)S(1)} async-done(((bf16[256,27,384]{2,0,1:T(8,128)(2,1)}), bf16[256,27,256]{2,0,1:T(8,128)(2,1)S(1)}, s32[]{:S(2)}) %slice-start.1) | async-done | bytes 3538968 | tf_op jit(solution)/shard_map/slice | solution.py:46
  73.7 2.3 %fusion.9 = f32[2,4,8,9,256]{4,2,3,1,0:T(8,128)S(1)} fusion(bf16[256,3,3,3,256]{4,0,3,2,1:T(8,128)(2,1)S(1)} %bitcast.55, bf16[4,6,1,7,1,256]{5,3,4,1,0,2:T(8,128)(2,1)S(1)} %get-tuple-element.18, bf16[4,6,1,7,1,256]{5,3,4,1,0,2:T(8,128)(2,1)S(1)} %get-tuple-element.17, bf16[4,6,1,8,9,256]{5,3,4,1,0,2:T(8,128)(2,1)S(1)} %fusion.6), kind=kOutput, calls=%fused_computation.15 | convolution fusion | flops 2043838464 | bytes 5185536 | tf_op jit(solution)/shard_map/conv_general_dilated | solution.py:18
  76.1 0.2 copy.55
  76.3 0.4 copy.56
  76.7 0.6 squeeze.2
  77.4 0.1 fusion.26
  77.5 12.2 %all_to_all.30 = bf16[2,16,16,256]{3,2,0,1:T(8,128)(2,1)S(1)} all-to-all(bf16[2,16,16,256]{3,2,0,1:T(8,128)(2,1)S(1)} %copy.57), channel_id=1, replica_groups=mesh['depth'=16,'filt'=16] {'filt'}, dimensions={1} | all-to-all | bytes 524288 | tf_op jit(solution)/shard_map/all_to_all | solution.py:104
  89.7 0.1 copy.58
  89.8 0.8 reshape.149
  (11 shorter events, 0.2 us)
Async XLA Ops:
  6.5 59.9 %all-gather.2.cloned.1.call-start = ((), (), s32[]{:S(2)}) async-start(), calls=%async_computation.2 | async-start | bytes 5640192 | tf_op jit(solution)/shard_map/all_gather | solution.py:42
  8.4 10.7 %collective-permute-start = (bf16[2,8,4096]{2,1,0:T(8,128)(2,1)}, bf16[2,8,4096]{2,1,0:T(8,128)(2,1)S(1)}, u32[]{:S(2)}, u32[]{:S(2)}) collective-permute-start(bf16[2,8,4096]{2,1,0:T(8,128)(2,1)} %param.7), channel_id=1, source_target_pairs={{0,16},{16,32},{32,48},{48,64},{64,80},{80,96},{96,112},{112,128},... | collective-permute-start | bytes 393224 | tf_op jit(solution)/shard_map/ppermute | solution.py:33
  11.9 8.1 %collective-permute-start.1 = (bf16[2,8,4096]{2,1,0:T(8,128)(2,1)}, bf16[2,8,4096]{2,1,0:T(8,128)(2,1)S(1)}, u32[]{:S(2)}, u32[]{:S(2)}) collective-permute-start(bf16[2,8,4096]{2,1,0:T(8,128)(2,1)} %param.7), channel_id=1, source_target_pairs={{16,0},{32,16},{48,32},{64,48},{80,64},{96,80},{112,96},{128,112},... | collective-permute-start | bytes 393224 | tf_op jit(solution)/shard_map/ppermute | solution.py:34
  26.9 33.1 %all-to-all-start = ((bf16[6,9,16,512]{3,0,1,2:T(8,128)(2,1)}), bf16[6,9,16,512]{3,0,1,2:T(8,128)(2,1)S(1)}, u32[]{:S(2)}, u32[]{:S(2)}) async-start(bf16[6,9,16,512]{3,0,1,2:T(8,128)(2,1)} %copy.50), calls=%async_computation | async-start | bytes 2359296 | tf_op jit(solution)/shard_map/all_to_all | solution.py:93
  65.5 0.9 copy-start
  66.5 1.5 %slice-start = ((bf16[256,27,384]{2,0,1:T(8,128)(2,1)}), bf16[256,27,128]{2,0,1:T(8,128)(2,1)S(1)}, s32[]{:S(2)}) async-start(bf16[256,27,384]{2,0,1:T(8,128)(2,1)} %all-gather.2.cloned.1.call-done), calls=%async_computation.3 | async-start | bytes 3538944 | tf_op jit(solution)/shard_map/slice | solution.py:45
  71.7 2.0 %slice-start.1 = ((bf16[256,27,384]{2,0,1:T(8,128)(2,1)}), bf16[256,27,256]{2,0,1:T(8,128)(2,1)S(1)}, s32[]{:S(2)}) async-start(bf16[256,27,384]{2,0,1:T(8,128)(2,1)} %all-gather.2.cloned.1.call-done), calls=%async_computation.4 | async-start | bytes 7077888 | tf_op jit(solution)/shard_map/slice | solution.py:46
Sparse Core Ops, SparseCore 0:
  9.2 57.2 all-gather.1

commit v8 on v5

--- a/solution.py
+++ b/solution.py
@@ -84,8 +84,8 @@
     grid = inside(planes * lax.axis_size("depth"), rows, planes, block_rows)
     hidden = jnp.where(grid, hidden, jnp.zeros_like(hidden))
     half = kernel_2.shape[0] // 2
-    second = jnp.concatenate([conv(hidden, kernel_2[:half]), conv(hidden, kernel_2[half:])], axis=1)
-    second = activate(second, bias_2)
+    pieces = lax.optimization_barrier((kernel_2[:half], kernel_2[half:]))
+    second = activate(conv(hidden, jnp.concatenate(pieces, axis=0)), bias_2)
 
     outs = second_kernel.shape[3]
     second = second.reshape(planes, count, outs, block_rows * SIDE)

time: 94.5 us -> 92.3 us (0.977)
  matrix products: 8.17 us -> 6.01 us
    conv_general_dilated x3 -> x2, matrix products: 8.17 us -> 6.01 us  [conv(): lax.conv_general_dilated(framed[None], kernel, (1, 1, 1), ((0, 0), (0, 0)...]
    concatenate x2 -> x0, local copies, waits for them, and re-layouts: 1.01 us -> none  [local(): jnp.concatenate([conv(hidden, kernel_2[:half]), conv(hidden, kernel_2[hal...]
  transfers between devices with their start and end apart: 5 -> 5, of which waited for: 2 -> 2; matrix products, arithmetic and copies ran while one was open for 10% -> 11% of each run, Pallas kernels for 0% -> 0%
where the time goes in v8:
time: 92.3 us; the launch traced here: 90.7 us
  waiting for transfers between devices  22.4 us (24%)
  starting transfers between devices  21.8 us (24%)
  between operations  13.6 us (15%)
  local copies, waits for them, and re-layouts  11.7 us (13%)
  blocking collectives  11.2 us (12%)
  matrix products  6.01 us (7%)
  other arithmetic  3.95 us (4%)
    all_to_all x1, waiting for transfers between devices, local(): mine = lax.all_to_all(windows, 'filt', 2, 1, tiled=True)  18.9 us
    all_to_all x1, blocking collectives, local(): result = lax.all_to_all(second, 'filt', 1, 3, tiled=True)  11.2 us
    all_to_all x1, starting transfers between devices, gather_biases(): whole = lax.all_to_all(spread, 'filt', 0, 0, tiled=True)  6.88 us
    conv_general_dilated x2, matrix products, conv(): lax.conv_general_dilated(framed[None], kernel, (1, 1, 1), ((0, 0), (0, 0)...  6.01 us
    all_to_all x1, starting transfers between devices, local(): mine = lax.all_to_all(windows, 'filt', 2, 1, tiled=True)  5.72 us
    ppermute x1, starting transfers between devices, depth_halo(): high = lax.ppermute(block[:reach], 'depth', backward)  5.63 us
    ppermute x1, starting transfers between devices, depth_halo(): low = lax.ppermute(block[block.shape[0] - reach:], 'depth', forward)  3.55 us
    all_gather x1, waiting for transfers between devices, gather_kernels(): lax.all_gather(jnp.concatenate([first, second], axis=2), 'filt', axis=0,...  3.45 us
  transfers between devices with their start and end apart: 5, of which 2 were waited for; matrix products, arithmetic and copies ran while one was open for 11% of the time, Pallas kernels for 0%

profile of v8, /device:TPU:17, one launch (start us, length us, event | category | flops | bytes accessed | tf_op | source)
XLA Modules:
  0.0 90.7 jit_solution(6804155593806783500)
XLA Ops:
  6.5 0.0 all-gather.2.cloned.1.call-start
  6.5 1.8 %pad_maximum_fusion.2 = bf16[16,27,384]{2,0,1:T(8,128)(2,1)} fusion(bf16[16,27,256]{2,0,1:T(8,128)(2,1)} %bitcast.56, bf16[16,27,128]{2,0,1:T(8,128)(2,1)} %bitcast.57), kind=kLoop, calls=%fused_computation.37 | loop fusion | flops 663552 | bytes 663552 | tf_op jit(solution)/shard_map/concatenate | solution.py:42
  8.3 0.0 all-gather.2.cloned.1.call-update
  8.3 3.5 %collective-permute-start = (bf16[2,8,4096]{2,1,0:T(8,128)(2,1)}, bf16[2,8,4096]{2,1,0:T(8,128)(2,1)S(1)}, u32[]{:S(2)}, u32[]{:S(2)}) collective-permute-start(bf16[2,8,4096]{2,1,0:T(8,128)(2,1)} %param.5), channel_id=1, source_target_pairs={{0,16},{16,32},{32,48},{48,64},{64,80},{80,96},{96,112},{112,128},... | collective-permute-start | bytes 393224 | tf_op jit(solution)/shard_map/ppermute | solution.py:33
  11.9 5.6 %collective-permute-start.1 = (bf16[2,8,4096]{2,1,0:T(8,128)(2,1)}, bf16[2,8,4096]{2,1,0:T(8,128)(2,1)S(1)}, u32[]{:S(2)}, u32[]{:S(2)}) collective-permute-start(bf16[2,8,4096]{2,1,0:T(8,128)(2,1)} %param.5), channel_id=1, source_target_pairs={{16,0},{32,16},{48,32},{64,48},{80,64},{96,80},{112,96},{128,112},... | collective-permute-start | bytes 393224 | tf_op jit(solution)/shard_map/ppermute | solution.py:34
  17.5 0.7 pad_maximum_fusion.3
  18.2 0.6 broadcast_in_dim.13
  18.8 6.9 %all-to-all-start.1 = ((f32[16,2,16]{2,1,0:T(2,128)}), f32[16,2,16]{2,1,0:T(2,128)S(1)}, u32[]{:S(2)}, u32[]{:S(2)}) async-start(f32[16,2,16]{2,1,0:T(2,128)} %broadcast_in_dim.13), calls=%async_computation.1 | async-start | bytes 32768 | tf_op jit(solution)/shard_map/all_to_all | solution.py:54
  25.7 0.0 collective-permute-done
  25.7 0.0 collective-permute-done.1
  25.7 1.0 %pad_maximum_fusion.1 = bf16[6,8,4096]{2,1,0:T(8,128)(2,1)S(1)} fusion(bf16[2,8,4096]{2,1,0:T(8,128)(2,1)S(1)} %collective-permute-done.1, bf16[2,8,4096]{2,1,0:T(8,128)(2,1)} %param.5, bf16[2,8,4096]{2,1,0:T(8,128)(2,1)S(1)} %collective-permute-done), kind=kLoop, calls=%fused_computation.36 | loop fusion | flops 393216 | bytes 786432 | tf_op jit(solution)/shard_map/concatenate | solution.py:35
  26.7 0.8 reshape.83
  27.5 0.7 pad_slice_fusion.1
  28.2 0.5 copy.37
  28.7 0.5 copy.38
  29.2 0.3 pad_maximum_fusion
  29.6 0.5 copy.49
  30.0 1.7 %reshape.106 = bf16[6,8,16,512]{3,1,0,2:T(8,128)(2,1)} reshape(bf16[6,8,16,8,64]{4,3,1,0,2:T(8,128)(2,1)S(1)} %copy.49) | data formatting | bytes 1572864 | tf_op jit(solution)/shard_map/reshape | solution.py:79
  31.7 0.0 all-to-all-done.1
  31.7 5.7 %all-to-all-start = ((bf16[6,8,16,512]{3,1,0,2:T(8,128)(2,1)}), bf16[6,8,16,512]{3,1,0,2:T(8,128)(2,1)S(1)}, u32[]{:S(2)}, u32[]{:S(2)}) async-start(bf16[6,8,16,512]{3,1,0,2:T(8,128)(2,1)} %reshape.106), calls=%async_computation | async-start | bytes 1572864 | tf_op jit(solution)/shard_map/all_to_all | solution.py:80
  37.5 0.1 broadcast_and_fusion
  37.6 0.1 add.50
  37.7 18.9 %all-to-all-done = bf16[6,8,16,512]{3,1,0,2:T(8,128)(2,1)S(1)} async-done(((bf16[6,8,16,512]{3,1,0,2:T(8,128)(2,1)}), bf16[6,8,16,512]{3,1,0,2:T(8,128)(2,1)S(1)}, u32[]{:S(2)}, u32[]{:S(2)}) %all-to-all-start) | async-done | bytes 786464 | tf_op jit(solution)/shard_map/all_to_all | solution.py:80
  56.5 0.1 copy.41
  56.6 0.8 reshape.101
  57.4 1.1 %copy.51 = bf16[6,128,8,1,64]{1,2,4,0,3:T(8,128)(2,1)S(1)} copy(bf16[6,128,8,1,64]{4,2,1,0,3:T(8,128)(2,1)S(1)} %reshape.101) | data formatting | bytes 1572864
  58.6 0.1 pad.5.clone
  58.6 0.1 copy.44
  58.8 0.1 slice.43
  58.8 0.0 copy-start
  58.8 3.5 %all-gather.2.cloned.1.call-done = bf16[256,27,384]{2,0,1:T(8,128)(2,1)} async-done(((bf16[16,27,384]{2,0,1:T(8,128)(2,1)}), bf16[256,27,384]{2,0,1:T(8,128)(2,1)}) %all-gather.2.cloned.1.call-update) | async-done | bytes 5308432 | tf_op jit(solution)/shard_map/all_gather | solution.py:42
  62.3 0.0 slice-start.2
  62.3 0.0 slice-start
  62.3 0.0 copy-done
  62.3 1.5 %slice-done.2 = bf16[256,27,128]{2,0,1:T(8,128)(2,1)S(1)} async-done(((bf16[256,27,384]{2,0,1:T(8,128)(2,1)}), bf16[256,27,128]{2,0,1:T(8,128)(2,1)S(1)}, s32[]{:S(2)}) %slice-start.2) | async-done | bytes 1769496 | tf_op jit(solution)/shard_map/slice | solution.py:45
  63.8 0.0 slice-start.1
  63.8 3.7 %fusion.10 = bf16[4,6,1,8,9,256]{5,3,4,1,0,2:T(8,128)(2,1)S(1)} fusion(bf16[256,3,3,3,128]{4,0,3,2,1:T(8,128)(2,1)S(1)} %bitcast.47, bf16[6,128,8,1,7,2]{1,4,5,2,0,3:T(8,128)(2,1)S(1)} %slice.43, bf16[6,128,8,1,8,9]{1,4,5,2,0,3:T(8,128)(2,1)S(1)} %copy.44, f32[256]{0:T(256)S(1)} %add.50, pred[8,9]{0,1:T(8,128)(4,1)S(1)} %copy-done, ...), kind=kOutput, calls=%fused_computation.16 | convolution fusion | flops 3064430592 | bytes 3712096 | tf_op jit(solution)/shard_map/conv_general_dilated | solution.py:18
  67.6 0.0 slice-done
  67.6 0.0 slice-done.1
  67.6 0.3 fusion.37
  67.9 2.3 %fusion = f32[2,4,8,9,256]{4,2,3,1,0:T(8,128)S(1)} fusion(bf16[128,3,3,3,256]{4,0,3,2,1:T(8,128)(2,1)S(1)} %bitcast.53, bf16[128,3,3,3,256]{4,0,3,2,1:T(8,128)(2,1)S(1)} %bitcast.54, bf16[4,6,1,7,1,256]{5,3,4,1,0,2:T(8,128)(2,1)S(1)} %get-tuple-element.12, bf16[4,6,1,7,1,256]{5,3,4,1,0,2:T(8,128)(2,1)S(1)} %get-tuple-element.11, ...), kind=kOutput, calls=%fused_computation.1 | convolution fusion | flops 2050916352 | bytes 5185536 | tf_op jit(solution)/shard_map/conv_general_dilated | solution.py:18
  70.2 0.2 copy.45
  70.5 0.4 copy.46
  70.9 0.6 squeeze.4
  71.5 0.1 fusion.29
  71.7 11.2 %all_to_all.35 = bf16[2,16,16,256]{3,2,0,1:T(8,128)(2,1)S(1)} all-to-all(bf16[2,16,16,256]{3,2,0,1:T(8,128)(2,1)S(1)} %copy.47), channel_id=1, replica_groups=mesh['depth'=16,'filt'=16] {'filt'}, dimensions={1} | all-to-all | bytes 524288 | tf_op jit(solution)/shard_map/all_to_all | solution.py:92
  82.9 0.1 copy.48
  83.0 0.8 reshape.90
  (7 shorter events, 0.1 us)
Async XLA Ops:
  6.5 55.8 %all-gather.2.cloned.1.call-start = ((), (), s32[]{:S(2)}) async-start(), calls=%async_computation.3 | async-start | bytes 5640192 | tf_op jit(solution)/shard_map/all_gather | solution.py:42
  8.3 17.4 %collective-permute-start = (bf16[2,8,4096]{2,1,0:T(8,128)(2,1)}, bf16[2,8,4096]{2,1,0:T(8,128)(2,1)S(1)}, u32[]{:S(2)}, u32[]{:S(2)}) collective-permute-start(bf16[2,8,4096]{2,1,0:T(8,128)(2,1)} %param.5), channel_id=1, source_target_pairs={{0,16},{16,32},{32,48},{48,64},{64,80},{80,96},{96,112},{112,128},... | collective-permute-start | bytes 393224 | tf_op jit(solution)/shard_map/ppermute | solution.py:33
  11.9 13.8 %collective-permute-start.1 = (bf16[2,8,4096]{2,1,0:T(8,128)(2,1)}, bf16[2,8,4096]{2,1,0:T(8,128)(2,1)S(1)}, u32[]{:S(2)}, u32[]{:S(2)}) collective-permute-start(bf16[2,8,4096]{2,1,0:T(8,128)(2,1)} %param.5), channel_id=1, source_target_pairs={{16,0},{32,16},{48,32},{64,48},{80,64},{96,80},{112,96},{128,112},... | collective-permute-start | bytes 393224 | tf_op jit(solution)/shard_map/ppermute | solution.py:34
  18.8 12.9 %all-to-all-start.1 = ((f32[16,2,16]{2,1,0:T(2,128)}), f32[16,2,16]{2,1,0:T(2,128)S(1)}, u32[]{:S(2)}, u32[]{:S(2)}) async-start(f32[16,2,16]{2,1,0:T(2,128)} %broadcast_in_dim.13), calls=%async_computation.1 | async-start | bytes 32768 | tf_op jit(solution)/shard_map/all_to_all | solution.py:54
  31.7 24.8 %all-to-all-start = ((bf16[6,8,16,512]{3,1,0,2:T(8,128)(2,1)}), bf16[6,8,16,512]{3,1,0,2:T(8,128)(2,1)S(1)}, u32[]{:S(2)}, u32[]{:S(2)}) async-start(bf16[6,8,16,512]{3,1,0,2:T(8,128)(2,1)} %reshape.106), calls=%async_computation | async-start | bytes 1572864 | tf_op jit(solution)/shard_map/all_to_all | solution.py:80
  58.8 3.5 %copy-start = (pred[8,9]{0,1:T(8,128)(4,1)S(1)}, pred[8,9]{0,1:T(8,128)(4,1)}, u32[]{:S(2)}) copy-start(pred[8,9]{0,1:T(8,128)(4,1)} %constant.42) | copy-start | bytes 220
  62.3 1.5 %slice-start.2 = ((bf16[256,27,384]{2,0,1:T(8,128)(2,1)}), bf16[256,27,128]{2,0,1:T(8,128)(2,1)S(1)}, s32[]{:S(2)}) async-start(bf16[256,27,384]{2,0,1:T(8,128)(2,1)} %all-gather.2.cloned.1.call-done), calls=%async_computation.6 | async-start | bytes 3538944 | tf_op jit(solution)/shard_map/slice | solution.py:45
  62.3 5.3 %slice-start = ((s8[5308416]{0:T(1024)(128)(4,1)}), s8[4194304]{0:T(1024)(128)(4,1)S(1)}, s32[]{:S(2)}) async-start(s8[5308416]{0:T(1024)(128)(4,1)} %bitcast.45), calls=%async_computation.4 | async-start | bytes 8388608
  63.8 3.8 %slice-start.1 = ((s8[5308416]{0:T(1024)(128)(4,1)}), s8[1114112]{0:T(1024)(128)(4,1)S(1)}, s32[]{:S(2)}) async-start(s8[5308416]{0:T(1024)(128)(4,1)} %bitcast.45), calls=%async_computation.5 | async-start | bytes 2228224
Sparse Core Ops, SparseCore 0:
  9.2 53.0 all-gather.1

commit v9 on v8

--- a/solution.py
+++ b/solution.py
@@ -80,7 +80,9 @@
     mine = lax.all_to_all(windows, "filt", 2, 1, tiled=True)
     mine = mine.reshape(planes + 4, count * chans, block_rows + 4, SIDE)
 
-    hidden = activate(conv(mine, kernel_1), bias_1)
+    half_1 = kernel_1.shape[0] // 2
+    pieces_1 = lax.optimization_barrier((kernel_1[:half_1], kernel_1[half_1:]))
+    hidden = activate(conv(mine, jnp.concatenate(pieces_1, axis=0)), bias_1)
     grid = inside(planes * lax.axis_size("depth"), rows, planes, block_rows)
     hidden = jnp.where(grid, hidden, jnp.zeros_like(hidden))
     half = kernel_2.shape[0] // 2

time: 92.3 us -> 92.6 us (level)
  no operation moved by 1% of the time
where the time goes in v9:
time: 92.6 us; the launch traced here: 90.9 us
  waiting for transfers between devices  22.3 us (24%)
  starting transfers between devices  21.8 us (24%)
  between operations  13.7 us (15%)
  local copies, waits for them, and re-layouts  12 us (13%)
  blocking collectives  11.2 us (12%)
  matrix products  6.02 us (7%)
  other arithmetic  3.97 us (4%)
    all_to_all x1, waiting for transfers between devices, local(): mine = lax.all_to_all(windows, 'filt', 2, 1, tiled=True)  18.9 us
    all_to_all x1, blocking collectives, local(): result = lax.all_to_all(second, 'filt', 1, 3, tiled=True)  11.2 us
    all_to_all x1, starting transfers between devices, gather_biases(): whole = lax.all_to_all(spread, 'filt', 0, 0, tiled=True)  6.88 us
    conv_general_dilated x2, matrix products, conv(): lax.conv_general_dilated(framed[None], kernel, (1, 1, 1), ((0, 0), (0, 0)...  6.02 us
    all_to_all x1, starting transfers between devices, local(): mine = lax.all_to_all(windows, 'filt', 2, 1, tiled=True)  5.72 us
    ppermute x1, starting transfers between devices, depth_halo(): high = lax.ppermute(block[:reach], 'depth', backward)  5.63 us
    ppermute x1, starting transfers between devices, depth_halo(): low = lax.ppermute(block[block.shape[0] - reach:], 'depth', forward)  3.55 us
    all_gather x1, waiting for transfers between devices, gather_kernels(): lax.all_gather(jnp.concatenate([first, second], axis=2), 'filt', axis=0,...  3.41 us
  transfers between devices with their start and end apart: 5, of which 2 were waited for; matrix products, arithmetic and copies ran while one was open for 11% of the time, Pallas kernels for 0%

profile of v9, /device:TPU:17, one launch (start us, length us, event | category | flops | bytes accessed | tf_op | source)
XLA Modules:
  0.0 90.9 jit_solution(7914376810451167111)
XLA Ops:
  6.5 0.0 all-gather.2.cloned.1.call-start
  6.5 1.8 %pad_maximum_fusion.2 = bf16[16,27,384]{2,0,1:T(8,128)(2,1)} fusion(bf16[16,27,256]{2,0,1:T(8,128)(2,1)} %bitcast.57, bf16[16,27,128]{2,0,1:T(8,128)(2,1)} %bitcast.58), kind=kLoop, calls=%fused_computation.41 | loop fusion | flops 663552 | bytes 663552 | tf_op jit(solution)/shard_map/concatenate | solution.py:42
  8.3 0.0 all-gather.2.cloned.1.call-update
  8.4 3.5 %collective-permute-start = (bf16[2,8,4096]{2,1,0:T(8,128)(2,1)}, bf16[2,8,4096]{2,1,0:T(8,128)(2,1)S(1)}, u32[]{:S(2)}, u32[]{:S(2)}) collective-permute-start(bf16[2,8,4096]{2,1,0:T(8,128)(2,1)} %param.5), channel_id=1, source_target_pairs={{0,16},{16,32},{32,48},{48,64},{64,80},{80,96},{96,112},{112,128},... | collective-permute-start | bytes 393224 | tf_op jit(solution)/shard_map/ppermute | solution.py:33
  11.9 5.6 %collective-permute-start.1 = (bf16[2,8,4096]{2,1,0:T(8,128)(2,1)}, bf16[2,8,4096]{2,1,0:T(8,128)(2,1)S(1)}, u32[]{:S(2)}, u32[]{:S(2)}) collective-permute-start(bf16[2,8,4096]{2,1,0:T(8,128)(2,1)} %param.5), channel_id=1, source_target_pairs={{16,0},{32,16},{48,32},{64,48},{80,64},{96,80},{112,96},{128,112},... | collective-permute-start | bytes 393224 | tf_op jit(solution)/shard_map/ppermute | solution.py:34
  17.6 0.7 pad_maximum_fusion.3
  18.2 0.6 broadcast_in_dim.13
  18.8 6.9 %all-to-all-start.1 = ((f32[16,2,16]{2,1,0:T(2,128)}), f32[16,2,16]{2,1,0:T(2,128)S(1)}, u32[]{:S(2)}, u32[]{:S(2)}) async-start(f32[16,2,16]{2,1,0:T(2,128)} %broadcast_in_dim.13), calls=%async_computation.1 | async-start | bytes 32768 | tf_op jit(solution)/shard_map/all_to_all | solution.py:54
  25.7 0.0 collective-permute-done
  25.7 0.0 collective-permute-done.1
  25.7 1.0 %pad_maximum_fusion.1 = bf16[6,8,4096]{2,1,0:T(8,128)(2,1)S(1)} fusion(bf16[2,8,4096]{2,1,0:T(8,128)(2,1)S(1)} %collective-permute-done.1, bf16[2,8,4096]{2,1,0:T(8,128)(2,1)} %param.5, bf16[2,8,4096]{2,1,0:T(8,128)(2,1)S(1)} %collective-permute-done), kind=kLoop, calls=%fused_computation.40 | loop fusion | flops 393216 | bytes 786432 | tf_op jit(solution)/shard_map/concatenate | solution.py:35
  26.7 0.8 reshape.83
  27.5 0.7 pad_slice_fusion.1
  28.2 0.5 copy.37
  28.7 0.5 copy.38
  29.3 0.3 pad_maximum_fusion
  29.6 0.5 copy.49
  30.1 1.7 %reshape.105 = bf16[6,8,16,512]{3,1,0,2:T(8,128)(2,1)} reshape(bf16[6,8,16,8,64]{4,3,1,0,2:T(8,128)(2,1)S(1)} %copy.49) | data formatting | bytes 1572864 | tf_op jit(solution)/shard_map/reshape | solution.py:79
  31.7 0.0 all-to-all-done.1
  31.7 5.7 %all-to-all-start = ((bf16[6,8,16,512]{3,1,0,2:T(8,128)(2,1)}), bf16[6,8,16,512]{3,1,0,2:T(8,128)(2,1)S(1)}, u32[]{:S(2)}, u32[]{:S(2)}) async-start(bf16[6,8,16,512]{3,1,0,2:T(8,128)(2,1)} %reshape.105), calls=%async_computation | async-start | bytes 1572864 | tf_op jit(solution)/shard_map/all_to_all | solution.py:80
  37.5 0.1 broadcast_and_fusion
  37.6 0.1 add.50
  37.7 18.9 %all-to-all-done = bf16[6,8,16,512]{3,1,0,2:T(8,128)(2,1)S(1)} async-done(((bf16[6,8,16,512]{3,1,0,2:T(8,128)(2,1)}), bf16[6,8,16,512]{3,1,0,2:T(8,128)(2,1)S(1)}, u32[]{:S(2)}, u32[]{:S(2)}) %all-to-all-start) | async-done | bytes 786464 | tf_op jit(solution)/shard_map/all_to_all | solution.py:80
  56.6 0.1 copy.41
  56.6 0.8 reshape.100
  57.5 1.1 %copy.51 = bf16[6,128,8,1,64]{1,2,4,0,3:T(8,128)(2,1)S(1)} copy(bf16[6,128,8,1,64]{4,2,1,0,3:T(8,128)(2,1)S(1)} %reshape.100) | data formatting | bytes 1572864
  58.6 0.1 pad.5.clone
  58.7 0.1 copy.44
  58.8 0.1 slice.58
  58.9 0.0 copy-start
  58.9 3.4 %all-gather.2.cloned.1.call-done = bf16[256,27,384]{2,0,1:T(8,128)(2,1)} async-done(((bf16[16,27,384]{2,0,1:T(8,128)(2,1)}), bf16[256,27,384]{2,0,1:T(8,128)(2,1)}) %all-gather.2.cloned.1.call-update) | async-done | bytes 5308432 | tf_op jit(solution)/shard_map/all_gather | solution.py:42
  62.3 0.0 slice-start
  62.3 1.7 %fusion.49 = (bf16[128,27,128]{2,0,1:T(8,128)(2,1)S(1)}, bf16[128,27,128]{2,0,1:T(8,128)(2,1)S(1)}) fusion(bf16[256,27,384]{2,0,1:T(8,128)(2,1)} %all-gather.2.cloned.1.call-done), kind=kLoop, calls=%fused_computation.54 | loop fusion | bytes 3538944 | tf_op jit(solution)/shard_map/slice | solution.py:84
  64.0 0.0 copy-done
  64.0 0.0 slice-start.1
  64.0 3.8 %fusion.20 = bf16[4,6,1,8,9,256]{5,3,4,1,0,2:T(8,128)(2,1)S(1)} fusion(bf16[128,3,3,3,128]{4,0,3,2,1:T(8,128)(2,1)S(1)} %bitcast.55, bf16[128,3,3,3,128]{4,0,3,2,1:T(8,128)(2,1)S(1)} %bitcast.56, bf16[6,128,8,1,7,2]{1,4,5,2,0,3:T(8,128)(2,1)S(1)} %slice.58, bf16[6,128,8,1,8,9]{1,4,5,2,0,3:T(8,128)(2,1)S(1)} %copy.44, f32[256]{0:T(256)S(1)} %add.50, ...), kind=kOutput, calls=%fused_computation.20 | convolution fusion | flops 3067969536 | bytes 3712096 | tf_op jit(solution)/shard_map/conv_general_dilated | solution.py:18
  67.8 0.0 slice-done
  67.8 0.0 slice-done.1
  67.8 0.3 fusion.50
  68.2 2.3 %fusion = f32[2,4,8,9,256]{4,2,3,1,0:T(8,128)S(1)} fusion(bf16[128,3,3,3,256]{4,0,3,2,1:T(8,128)(2,1)S(1)} %bitcast.52, bf16[128,3,3,3,256]{4,0,3,2,1:T(8,128)(2,1)S(1)} %bitcast.53, bf16[4,6,1,7,1,256]{5,3,4,1,0,2:T(8,128)(2,1)S(1)} %get-tuple-element.18, bf16[4,6,1,7,1,256]{5,3,4,1,0,2:T(8,128)(2,1)S(1)} %get-tuple-element.17, ...), kind=kOutput, calls=%fused_computation.1 | convolution fusion | flops 2050916352 | bytes 5185536 | tf_op jit(solution)/shard_map/conv_general_dilated | solution.py:18
  70.4 0.2 copy.45
  70.7 0.4 copy.46
  71.1 0.6 squeeze.4
  71.7 0.1 fusion.41
  71.9 11.2 %all_to_all.35 = bf16[2,16,16,256]{3,2,0,1:T(8,128)(2,1)S(1)} all-to-all(bf16[2,16,16,256]{3,2,0,1:T(8,128)(2,1)S(1)} %copy.47), channel_id=1, replica_groups=mesh['depth'=16,'filt'=16] {'filt'}, dimensions={1} | all-to-all | bytes 524288 | tf_op jit(solution)/shard_map/all_to_all | solution.py:94
  83.1 0.1 copy.48
  83.3 0.8 reshape.89
  (7 shorter events, 0.1 us)
Async XLA Ops:
  6.5 55.8 %all-gather.2.cloned.1.call-start = ((), (), s32[]{:S(2)}) async-start(), calls=%async_computation.3 | async-start | bytes 5640192 | tf_op jit(solution)/shard_map/all_gather | solution.py:42
  8.4 17.4 %collective-permute-start = (bf16[2,8,4096]{2,1,0:T(8,128)(2,1)}, bf16[2,8,4096]{2,1,0:T(8,128)(2,1)S(1)}, u32[]{:S(2)}, u32[]{:S(2)}) collective-permute-start(bf16[2,8,4096]{2,1,0:T(8,128)(2,1)} %param.5), channel_id=1, source_target_pairs={{0,16},{16,32},{32,48},{48,64},{64,80},{80,96},{96,112},{112,128},... | collective-permute-start | bytes 393224 | tf_op jit(solution)/shard_map/ppermute | solution.py:33
  11.9 13.8 %collective-permute-start.1 = (bf16[2,8,4096]{2,1,0:T(8,128)(2,1)}, bf16[2,8,4096]{2,1,0:T(8,128)(2,1)S(1)}, u32[]{:S(2)}, u32[]{:S(2)}) collective-permute-start(bf16[2,8,4096]{2,1,0:T(8,128)(2,1)} %param.5), channel_id=1, source_target_pairs={{16,0},{32,16},{48,32},{64,48},{80,64},{96,80},{112,96},{128,112},... | collective-permute-start | bytes 393224 | tf_op jit(solution)/shard_map/ppermute | solution.py:34
  18.8 12.9 %all-to-all-start.1 = ((f32[16,2,16]{2,1,0:T(2,128)}), f32[16,2,16]{2,1,0:T(2,128)S(1)}, u32[]{:S(2)}, u32[]{:S(2)}) async-start(f32[16,2,16]{2,1,0:T(2,128)} %broadcast_in_dim.13), calls=%async_computation.1 | async-start | bytes 32768 | tf_op jit(solution)/shard_map/all_to_all | solution.py:54
  31.7 24.8 %all-to-all-start = ((bf16[6,8,16,512]{3,1,0,2:T(8,128)(2,1)}), bf16[6,8,16,512]{3,1,0,2:T(8,128)(2,1)S(1)}, u32[]{:S(2)}, u32[]{:S(2)}) async-start(bf16[6,8,16,512]{3,1,0,2:T(8,128)(2,1)} %reshape.105), calls=%async_computation | async-start | bytes 1572864 | tf_op jit(solution)/shard_map/all_to_all | solution.py:80
  58.9 5.1 %copy-start = (pred[8,9]{0,1:T(8,128)(4,1)S(1)}, pred[8,9]{0,1:T(8,128)(4,1)}, u32[]{:S(2)}) copy-start(pred[8,9]{0,1:T(8,128)(4,1)} %constant.42) | copy-start | bytes 220
  62.3 5.5 %slice-start = ((s8[5308416]{0:T(1024)(128)(4,1)}), s8[4194304]{0:T(1024)(128)(4,1)S(1)}, s32[]{:S(2)}) async-start(s8[5308416]{0:T(1024)(128)(4,1)} %bitcast.45), calls=%async_computation.4 | async-start | bytes 8388608
  64.0 3.8 %slice-start.1 = ((s8[5308416]{0:T(1024)(128)(4,1)}), s8[1114112]{0:T(1024)(128)(4,1)S(1)}, s32[]{:S(2)}) async-start(s8[5308416]{0:T(1024)(128)(4,1)} %bitcast.45), calls=%async_computation.5 | async-start | bytes 2228224
Sparse Core Ops, SparseCore 0:
  9.2 53.0 all-gather.1
